TPU v7x, 32 devices: a whole 2x2x4 slice. The times are simulated.
32 devices in a mesh: rep: 8 (over z, x), tile: 4 (over y, core).
Axes of the slice: x: 2, y: 2, z: 4, core: 2. Of those that a mesh axis runs over, the one named last changes fastest.
Arguments:
- features: bfloat16 [16, 48, 72, 1536], P('rep', 'tile'), may hold values from -6 to 6
- conv_out: bfloat16 [16, 48, 72, 256], P('rep', 'tile'), may hold values from -6 to 6
- conv_weight: bfloat16 [9, 1536, 256], replicated, may hold values from -0.0546875 to 0.0546875
- norm_gain_vector: float32 [256], replicated, may hold values from 0.5 to 1.5
- norm_shift_vector: float32 [256], replicated, may hold values from -3 to 3
- class_map: float32 [3, 256], replicated, may hold values from -3 to 3
- labels: int32 [16, 48, 72], P('rep', 'tile'), may hold values from 0 to 2
- class_weight: int32 [3], replicated, may hold values from 1 to 39
Outputs:
- grad_features: bfloat16 [16, 48, 72, 1536], P('rep', 'tile')
- grad_weight: float32 [1536, 9, 256], P(('rep', 'tile'))
- grad_gain: float32 [256], replicated
- grad_shift: float32 [256], replicated
- grad_class: float32 [3, 256], replicated
- loss: float32 [], replicated
All inputs are finite; a program needn't handle non-finite values.
Results may differ from a plain program's by a relative error of at most 0.0049.
Values may be sent and summed in bfloat16 or wider, within the bound.
No kernel may reach another device: no remote copies, remote signals or barrier semaphores. Data moves between devices by JAX's collectives and lax.ppermute only.
A program may use at most 256 MiB of HBM per device.

v0:
```python
import jax
import jax.numpy as jnp
from jax import lax
from jax.sharding import PartitionSpec as P

IMG_DEV = 2
H = 48
W = 72
RATE = 12


def padded(x, sides, width):
    for axis, dim in sides:
        size, length = (lax.axis_size(axis), x.shape[dim])
        up = [(i, (i + 1) % size) for i in range(size - 1)]
        down = [(j, i) for i, j in up]
        last = lax.slice_in_dim(x, length - width, length, axis=dim)
        first = lax.slice_in_dim(x, 0, width, axis=dim)
        before = lax.ppermute(last, axis, up)
        after = lax.ppermute(first, axis, down)
        x = jnp.concatenate([before, x, after], axis=dim)
    return x


def body(
    features,
    conv_out,
    conv_weight,
    norm_gain_vector,
    norm_shift_vector,
    class_map,
    labels,
    class_weight,
):
    highest = lax.Precision.HIGHEST
    images, tile_rows, columns, in_chans = features.shape
    out_chans = conv_out.shape[3]
    local_pix = images * tile_rows * columns
    per_replica_part = IMG_DEV * H * W
    all_pix = lax.axis_size("rep") * per_replica_part
    yvals = conv_out.astype(jnp.float32).reshape(local_pix, out_chans)
    column_sum = lax.psum(jnp.sum(yvals, 0), "tile")
    centre_offset = yvals - column_sum / per_replica_part
    variance = lax.psum(jnp.sum(centre_offset * centre_offset, 0), "tile") / per_replica_part
    inverse_deviation = lax.rsqrt(variance + 1e-05)
    normalized_input = centre_offset * inverse_deviation
    preactivation_values = norm_gain_vector * normalized_input + norm_shift_vector
    zvals = jnp.maximum(preactivation_values, 0.0)
    logits = jnp.dot(zvals, class_map.T, precision=highest)
    onehot = (
        labels.reshape(local_pix, 1) == jnp.arange(class_map.shape[0], dtype=jnp.int32)
    ).astype(jnp.float32)
    weights_pix = jnp.sum(onehot * class_weight.astype(jnp.float32), -1)
    top_val = jnp.max(logits, -1, keepdims=True)
    log_total = top_val[:, 0] + jnp.log(jnp.sum(jnp.exp(logits - top_val), -1))
    cross = log_total - jnp.sum(onehot * logits, -1)
    weight_total, loss_total = lax.psum(
        (jnp.sum(weights_pix), jnp.sum(weights_pix * cross)), ("rep", "tile")
    )
    mean_weight = weight_total / all_pix
    loss = loss_total / mean_weight / all_pix
    probs = jnp.exp(logits - log_total[:, None])
    grad_logit = (weights_pix / mean_weight)[:, None] * (probs - onehot)
    class_local_slice = jnp.dot(grad_logit.T, zvals, precision=highest)
    grad_z = jnp.dot(grad_logit, class_map, precision=highest)
    preactivation_gradient = jnp.where(preactivation_values > 0, grad_z, 0.0)
    first_gradient_sum, second_gradient_sum, class_tile = lax.psum(
        (
            jnp.sum(preactivation_gradient, 0),
            jnp.sum(preactivation_gradient * normalized_input, 0),
            class_local_slice,
        ),
        "tile",
    )
    grad_shift, grad_gain, grad_class = lax.psum(
        (first_gradient_sum, second_gradient_sum, class_tile), "rep"
    )
    normalized_output_gradient = (
        norm_gain_vector
        * inverse_deviation
        * (
            preactivation_gradient
            - first_gradient_sum / per_replica_part
            - normalized_input * second_gradient_sum / per_replica_part
        )
    ).astype(jnp.bfloat16)
    normalized_output_gradient = normalized_output_gradient.reshape(
        images, tile_rows, columns, out_chans
    )
    extended = padded(normalized_output_gradient, (("tile", 1),), RATE)
    extended = jnp.pad(extended, ((0, 0), (0, 0), (RATE, RATE), (0, 0)))
    shifted_list = []
    for tap_index in range(9):
        row_off = RATE - (tap_index // 3 - 1) * RATE
        col_off = RATE - (tap_index % 3 - 1) * RATE
        piece = extended[:, row_off : row_off + tile_rows, col_off : col_off + columns, :]
        shifted_list.append(piece.reshape(local_pix, out_chans))
    accum_grad = jnp.zeros((local_pix, in_chans), jnp.float32)
    for tap_index in range(9):
        accum_grad = accum_grad + lax.dot_general(
            shifted_list[tap_index],
            conv_weight[tap_index],
            (((1,), (1,)), ((), ())),
            preferred_element_type=jnp.float32,
        )
    grad_features = accum_grad.astype(jnp.bfloat16).reshape(images, tile_rows, columns, in_chans)
    flat_x = features.reshape(local_pix, in_chans)
    parts_list = [
        lax.dot_general(
            flat_x, shifted, (((0,), (0,)), ((), ())), preferred_element_type=jnp.float32
        )
        for shifted in shifted_list
    ]
    grad_weight = lax.psum_scatter(
        jnp.stack(parts_list, 1), ("rep", "tile"), scatter_dimension=0, tiled=True
    )
    return (grad_features, grad_weight, grad_gain, grad_shift, grad_class, loss)


def solution(mesh):
    in_specs = (
        P("rep", "tile", None, None),
        P("rep", "tile", None, None),
        P(),
        P(),
        P(),
        P(),
        P("rep", "tile", None),
        P(),
    )
    out_specs = (P("rep", "tile", None, None), P(("rep", "tile"), None, None), P(), P(), P(), P())
    return jax.shard_map(body, mesh=mesh, in_specs=in_specs, out_specs=out_specs, check_vma=False)
```

profile of v0, /device:TPU:0, one launch (start us, length us, event | category | flops | bytes accessed | tf_op | source)
XLA Modules:
  0.0 405.0 jit_solution(10787423601491690530)
XLA Ops:
  8.7 8.4 %psum.70 = f32[256]{0:T(256)S(1)} all-reduce(f32[256]{0:T(256)S(1)} %convert_reduce_fusion), channel_id=1, replica_groups=mesh['rep'=8,'tile'=4] {'tile'}, use_global_device_ids=true, to_apply=%region_1.0 | all-reduce | flops 256 | bytes 2048 | tf_op jit(solution)/shard_map/psum | solution.py:42
  18.5 5.8 %psum.71 = f32[256]{0:T(256)S(1)} all-reduce(f32[256]{0:T(256)S(1)} %multiply_reduce_fusion.1), channel_id=1, replica_groups=mesh['rep'=8,'tile'=4] {'tile'}, use_global_device_ids=true, to_apply=%region_3.0 | all-reduce | flops 256 | bytes 2048 | tf_op jit(solution)/shard_map/psum | solution.py:44
  31.5 39.9 %all-reduce.1 = (f32[]{:T(128)}, f32[]{:T(128)}) all-reduce(f32[]{:T(128)} %get-tuple-element.31, f32[]{:T(128)} %get-tuple-element.40), channel_id=1, replica_groups=mesh['rep'=8,'tile'=4] {'rep','tile'}, use_global_device_ids=true, to_apply=%region_6.0 | all-reduce | flops 2 | bytes 16 | tf_op jit(solution)/shard_map/psum | solution.py:57
  73.1 4.6 %fusion.61 = (f32[256]{0:T(256)S(1)}, f32[256]{0:T(256)S(1)}, f32[1728,256]{1,0:T(8,128)}) fusion(f32[256]{0:T(256)S(1)} %get-tuple-element.49, f32[256]{0:T(256)S(1)} %broadcast_multiply_fusion.1, bf16[2,12,72,256]{3,2,1,0:T(8,128)(2,1)} %param.9, f32[3,256]{1,0:T(4,128)S(1)} %copy-done, f32[1728,3]{0,1:T(4,128)S(1)} %get-tuple-element.51, ...), kind=kOutput, calls=%fused_computation.92 | convolution fusion | flops 20374336 | bytes 4474368 | tf_op jit(solution)/shard_map/dot_general | solution.py:65
  77.6 6.9 %all-reduce.3 = (f32[256]{0:T(256)S(1)}, f32[256]{0:T(256)S(1)}, f32[3,256]{1,0:T(4,128)S(1)}) all-reduce(f32[256]{0:T(256)S(1)} %get-tuple-element.25, f32[256]{0:T(256)S(1)} %get-tuple-element.24, f32[3,256]{1,0:T(4,128)S(1)} %fusion.16), channel_id=1, replica_groups=mesh['rep'=8,'tile'=4] {'tile'}, use_global_device_ids=true, to_apply=%region_12.13 | all-reduce | flops 1280 | bytes 10240 | tf_op jit(solution)/shard_map/psum | solution.py:67
  90.4 3.8 collective-permute-done.1
  96.1 2.8 fusion.14
  101.7 2.8 fusion.12
  104.4 2.8 fusion.11
  107.2 2.8 fusion.10
  110.0 2.8 fusion.9
  115.5 2.8 fusion.7
  121.0 19.0 %copy.18 = f32[1536,9,256]{2,1,0:T(8,128)} copy(f32[1536,9,256]{0,2,1:T(8,128)} %fusion.6) | data formatting | bytes 28311552 | tf_op jit(solution)/shard_map/stack | solution.py:115
  140.7 21.3 %all-reduce.2 = (f32[256]{0:T(256)}, f32[256]{0:T(256)}, f32[3,256]{1,0:T(4,128)}) all-reduce(f32[256]{0:T(256)S(1)} %get-tuple-element.37, f32[256]{0:T(256)S(1)} %get-tuple-element.38, f32[3,256]{1,0:T(4,128)S(1)} %get-tuple-element.39), channel_id=1, replica_groups=mesh['rep'=8,'tile'=4] {'rep'}, use_global_device_ids=true, to_apply=%region_14.15 | all-reduce | flops 1280 | bytes 10240 | tf_op jit(solution)/shard_map/psum | solution.py:75
  162.0 7.7 %fusion.33 = f32[1728,1536]{1,0:T(8,128)} fusion(bf16[1728,256]{1,0:T(8,128)(2,1)S(1)} %multiply_convert_fusion, bf16[9,1536,256]{2,1,0:T(8,128)(2,1)} %param.10), kind=kOutput, calls=%fused_computation.52 | convolution fusion | flops 1358954496 | bytes 12288000 | tf_op jit(solution)/shard_map/dot_general | solution.py:100
  170.3 8.2 %fusion.26 = f32[1728,1536]{1,0:T(8,128)} fusion(bf16[1728,256]{1,0:T(8,128)(2,1)S(1)} %bitcast.174, bf16[9,1536,256]{2,1,0:T(8,128)(2,1)} %param.10), kind=kOutput, calls=%fused_computation.45 | convolution fusion | flops 1358954496 | bytes 12288000 | tf_op jit(solution)/shard_map/dot_general | solution.py:100
  178.5 6.4 %fusion.29 = f32[1728,1536]{1,0:T(8,128)} fusion(bf16[1728,256]{1,0:T(8,128)(2,1)S(1)} %bitcast.173, bf16[9,1536,256]{2,1,0:T(8,128)(2,1)S(1)} %bitcast.167), kind=kOutput, calls=%fused_computation.48 | convolution fusion | flops 1358954496 | bytes 12288000 | tf_op jit(solution)/shard_map/dot_general | solution.py:100
  184.9 6.3 %fusion.31 = f32[1728,1536]{1,0:T(8,128)} fusion(bf16[1728,256]{1,0:T(8,128)(2,1)S(1)} %bitcast.172, bf16[9,1536,256]{2,1,0:T(8,128)(2,1)S(1)} %bitcast.167), kind=kOutput, calls=%fused_computation.50 | convolution fusion | flops 1358954496 | bytes 12288000 | tf_op jit(solution)/shard_map/dot_general | solution.py:100
  191.2 6.3 %fusion.35 = f32[1728,1536]{1,0:T(8,128)} fusion(bf16[1728,256]{1,0:T(8,128)(2,1)S(1)} %bitcast.171, bf16[9,1536,256]{2,1,0:T(8,128)(2,1)S(1)} %bitcast.167), kind=kOutput, calls=%fused_computation.54 | convolution fusion | flops 1358954496 | bytes 12288000 | tf_op jit(solution)/shard_map/dot_general | solution.py:100
  197.6 5.7 %fusion.37 = f32[1728,1536]{1,0:T(8,128)} fusion(bf16[1728,256]{1,0:T(8,128)(2,1)S(1)} %bitcast.170, bf16[9,1536,256]{2,1,0:T(8,128)(2,1)S(1)} %bitcast.167), kind=kOutput, calls=%fused_computation.56 | convolution fusion | flops 1358954496 | bytes 12288000 | tf_op jit(solution)/shard_map/dot_general | solution.py:100
  203.3 5.6 %fusion.41 = f32[1728,1536]{1,0:T(8,128)} fusion(bf16[1728,256]{1,0:T(8,128)(2,1)S(1)} %bitcast.169, bf16[9,1536,256]{2,1,0:T(8,128)(2,1)S(1)} %bitcast.167), kind=kOutput, calls=%fused_computation.60 | convolution fusion | flops 1358954496 | bytes 12288000 | tf_op jit(solution)/shard_map/dot_general | solution.py:100
  209.0 6.2 %fusion.39 = f32[1728,1536]{1,0:T(8,128)} fusion(bf16[1728,256]{1,0:T(8,128)(2,1)S(1)} %bitcast.164, bf16[9,1536,256]{2,1,0:T(8,128)(2,1)S(1)} %bitcast.167), kind=kOutput, calls=%fused_computation.58 | convolution fusion | flops 1358954496 | bytes 12288000 | tf_op jit(solution)/shard_map/dot_general | solution.py:100
  215.1 30.1 %add_convert_fusion = bf16[1728,1536]{1,0:T(8,128)(2,1)} fusion(f32[1728,1536]{1,0:T(8,128)} %fusion.26, f32[1728,1536]{1,0:T(8,128)} %fusion.29, f32[1728,1536]{1,0:T(8,128)} %fusion.31, f32[1728,1536]{1,0:T(8,128)} %fusion.33, f32[1728,1536]{1,0:T(8,128)} %fusion.35, f32[1728,1536]{1,0:T(8,128)} %fusion.37, f32[1728,1536]{1,0:T(8,128)} %fusion.41, ...), kind=kOutput, calls=%fused_computation.2 | convolution fusion | flops 1382842368 | bytes 91914240 | tf_op jit(solution)/shard_map/dot_general | solution.py:100
  245.2 149.6 %reduce-scatter.2.cloned.1.call-done = f32[48,9,256]{2,1,0:T(8,128)} async-done(((f32[1536,9,256]{2,1,0:T(8,128)}), f32[48,9,256]{2,1,0:T(8,128)}) %reduce-scatter.2.cloned.1.call-update) | async-done | bytes 442384 | tf_op jit(solution)/shard_map/reduce_scatter | solution.py:114
  (52 shorter events, 29.9 us)
Async XLA Ops:
  7.2 20.6 %copy-start = (f32[3,256]{1,0:T(4,128)S(1)}, f32[3,256]{1,0:T(4,128)}, u32[]{:S(2)}) copy-start(f32[3,256]{1,0:T(4,128)} %param.13) | copy-start | bytes 9220
  7.2 64.9 %copy-start.6 = (f32[256]{0:T(256)S(1)}, f32[256]{0:T(256)}, u32[]{:S(2)}) copy-start(f32[256]{0:T(256)} %param.11) | copy-start | bytes 3076
  7.2 64.9 %copy-start.7 = (f32[256]{0:T(256)S(1)}, f32[256]{0:T(256)}, u32[]{:S(2)}) copy-start(f32[256]{0:T(256)} %param.12) | copy-start | bytes 3076
  7.2 387.6 %reduce-scatter.2.cloned.1.call-start = ((), (), s32[]{:S(2)}) async-start(), calls=%async_computation.1 | async-start | bytes 25952256 | tf_op jit(solution)/shard_map/reduce_scatter | solution.py:114
  73.1 23.0 %slice-start = ((s8[5308416]{0:T(1024)(128)(4,1)}), s8[1114112]{0:T(1024)(128)(4,1)S(1)}, s32[]{:S(2)}) async-start(s8[5308416]{0:T(1024)(128)(4,1)} %bitcast.158), calls=%async_computation.2 | async-start | bytes 2228224
  84.5 11.5 %slice-start.1 = ((s8[5308416]{0:T(1024)(128)(4,1)}), s8[4194304]{0:T(1024)(128)(4,1)S(1)}, s32[]{:S(2)}) async-start(s8[5308416]{0:T(1024)(128)(4,1)} %bitcast.158), calls=%async_computation.3 | async-start | bytes 8388608
  86.9 3.5 collective-permute-start
  88.4 5.8 %collective-permute-start.1 = (bf16[2,12,72,256]{3,2,1,0:T(8,128)(2,1)S(1)}, bf16[2,12,72,256]{3,2,1,0:T(8,128)(2,1)S(1)}, u32[]{:S(2)}, u32[]{:S(2)}) collective-permute-start(bf16[2,12,72,256]{3,2,1,0:T(8,128)(2,1)S(1)} %bitcast.161), channel_id=1, source_target_pairs={{1,0},{2,1},{3,2},{5,4},{6,5},{7,6},{9,8},{10,9},{11,10},{13,12},{... | collective-permute-start | bytes 2654216 | tf_op jit(solution)/shard_map/ppermute | solution.py:20
  90.4 25.1 %copy-start.4 = (bf16[2,12,72,256]{3,2,1,0:T(8,128)(2,1)}, bf16[2,12,72,256]{3,2,1,0:T(8,128)(2,1)S(1)}, u32[]{:S(2)}) copy-start(bf16[2,12,72,256]{3,2,1,0:T(8,128)(2,1)S(1)} %collective-permute-done) | copy-start | bytes 2654212
  96.0 22.2 %copy-start.2 = (bf16[2,36,96,256]{3,2,1,0:T(8,128)(2,1)}, bf16[2,36,96,256]{3,2,1,0:T(8,128)(2,1)S(1)}, u32[]{:S(2)}) copy-start(bf16[2,36,96,256]{3,2,1,0:T(8,128)(2,1)S(1)} %fusion.5) | copy-start | bytes 10616836
  162.0 7.7 %copy-start.3 = (bf16[2,36,96,256]{3,2,1,0:T(8,128)(2,1)S(1)}, bf16[2,36,96,256]{3,2,1,0:T(8,128)(2,1)}, u32[]{:S(2)}) copy-start(bf16[2,36,96,256]{3,2,1,0:T(8,128)(2,1)} %copy-done.2) | copy-start | bytes 10616836
  169.7 8.8 %slice-start.2 = ((s8[7077888]{0:T(1024)(128)(4,1)}), s8[2883584]{0:T(1024)(128)(4,1)S(1)}, s32[]{:S(2)}) async-start(s8[7077888]{0:T(1024)(128)(4,1)} %bitcast.166), calls=%async_computation.4 | async-start | bytes 5767168
  170.3 8.2 %slice-start.3 = ((s8[7077888]{0:T(1024)(128)(4,1)}), s8[4194304]{0:T(1024)(128)(4,1)S(1)}, s32[]{:S(2)}) async-start(s8[7077888]{0:T(1024)(128)(4,1)} %bitcast.166), calls=%async_computation.5 | async-start | bytes 8388608
  208.9 6.2 %copy-start.5 = (bf16[2,12,72,256]{3,2,1,0:T(8,128)(2,1)S(1)}, bf16[2,12,72,256]{3,2,1,0:T(8,128)(2,1)}, u32[]{:S(2)}) copy-start(bf16[2,12,72,256]{3,2,1,0:T(8,128)(2,1)} %copy-done.4) | copy-start | bytes 2654212
  215.1 181.9 %copy-start.1 = (f32[3,256]{1,0:T(4,128)S(1)}, f32[3,256]{1,0:T(4,128)}, u32[]{:S(2)}) copy-start(f32[3,256]{1,0:T(4,128)} %param.13) | copy-start | bytes 9220
Sparse Core Ops, SparseCore 0:
  140.1 254.6 reduce-scatter.1
where the time goes:
time: 406 us; the launch traced here: 405 us
  waiting for transfers between devices  154 us (38%)
  matrix products  116 us (29%)
  blocking collectives  82.2 us (20%)
  local copies, waits for them, and re-layouts  22.6 us (6%)
  between operations  16.6 us (4%)
  other arithmetic  11.1 us (3%)
    reduce_scatter x1, waiting for transfers between devices, body(): lax.psum_scatter(jnp.stack(parts_list, 1), ('rep', 'tile'), scatter_dimen...  150 us
    dot_general x9, matrix products, body(): lax.dot_general(shifted_list[tap_index], conv_weight[tap_index], (((1,),...  82.6 us
    psum x1, blocking collectives, body(): lax.psum((jnp.sum(weights_pix), jnp.sum(weights_pix * cross)), ('rep', 't...  39.9 us
    dot_general x9, matrix products, body(): lax.dot_general(flat_x, shifted, (((0,), (0,)), ((), ())), preferred_elem...  25 us
    psum x1, blocking collectives, body(): lax.psum((first_gradient_sum, second_gradient_sum, class_tile), 'rep')  21.3 us
    another operation x1, local copies, waits for them, and re-layouts, body(): jnp.stack(parts_list, 1)  19 us
    psum x1, blocking collectives, body(): column_sum = lax.psum(jnp.sum(yvals, 0), 'tile')  8.36 us
  transfers between devices with their start and end apart: 3, of which 3 were waited for; matrix products, arithmetic and copies ran while one was open for 21% of the time, Pallas kernels for 0%

commit v1 on v0

--- a/solution.py
+++ b/solution.py
@@ -22,6 +22,37 @@
     return x
 
 
+def index_bits(axes):
+    bits = []
+    for axis in reversed(axes):
+        size = lax.axis_size(axis)
+        assert size & (size - 1) == 0
+        bits += [(axis, b) for b in range(size.bit_length() - 1)]
+    return bits
+
+
+def exchange(x, axis, bit):
+    size = lax.axis_size(axis)
+    pairs = [(i, i ^ (1 << bit)) for i in range(size)]
+    return lax.ppermute(x, axis, pairs)
+
+
+def butterfly_sum(x, axes):
+    for axis, bit in index_bits(axes):
+        x = jax.tree.map(lambda v, w: v + w, x, exchange(x, axis, bit))
+    return x
+
+
+def halving_scatter(x, axes):
+    for axis, bit in index_bits(axes):
+        mine = (lax.axis_index(axis) >> bit) & 1
+        x = x.reshape((2, x.shape[0] // 2) + x.shape[1:])
+        keep = lax.dynamic_index_in_dim(x, mine, 0, keepdims=False)
+        send = lax.dynamic_index_in_dim(x, 1 - mine, 0, keepdims=False)
+        x = keep + exchange(send, axis, bit)
+    return x
+
+
 def body(
     features,
     conv_out,
@@ -35,9 +66,18 @@
     highest = lax.Precision.HIGHEST
     images, tile_rows, columns, in_chans = features.shape
     out_chans = conv_out.shape[3]
+    taps = conv_weight.shape[0]
     local_pix = images * tile_rows * columns
     per_replica_part = IMG_DEV * H * W
     all_pix = lax.axis_size("rep") * per_replica_part
+    classes = class_map.shape[0]
+
+    onehot = (
+        labels.reshape(local_pix, 1) == jnp.arange(classes, dtype=jnp.int32)
+    ).astype(jnp.float32)
+    weights_pix = jnp.sum(onehot * class_weight.astype(jnp.float32), -1)
+    weight_total = butterfly_sum(jnp.sum(weights_pix), ("rep", "tile"))
+
     yvals = conv_out.astype(jnp.float32).reshape(local_pix, out_chans)
     column_sum = lax.psum(jnp.sum(yvals, 0), "tile")
     centre_offset = yvals - column_sum / per_replica_part
@@ -47,34 +87,28 @@
     preactivation_values = norm_gain_vector * normalized_input + norm_shift_vector
     zvals = jnp.maximum(preactivation_values, 0.0)
     logits = jnp.dot(zvals, class_map.T, precision=highest)
-    onehot = (
-        labels.reshape(local_pix, 1) == jnp.arange(class_map.shape[0], dtype=jnp.int32)
-    ).astype(jnp.float32)
-    weights_pix = jnp.sum(onehot * class_weight.astype(jnp.float32), -1)
     top_val = jnp.max(logits, -1, keepdims=True)
     log_total = top_val[:, 0] + jnp.log(jnp.sum(jnp.exp(logits - top_val), -1))
     cross = log_total - jnp.sum(onehot * logits, -1)
-    weight_total, loss_total = lax.psum(
-        (jnp.sum(weights_pix), jnp.sum(weights_pix * cross)), ("rep", "tile")
-    )
     mean_weight = weight_total / all_pix
-    loss = loss_total / mean_weight / all_pix
     probs = jnp.exp(logits - log_total[:, None])
     grad_logit = (weights_pix / mean_weight)[:, None] * (probs - onehot)
     class_local_slice = jnp.dot(grad_logit.T, zvals, precision=highest)
     grad_z = jnp.dot(grad_logit, class_map, precision=highest)
     preactivation_gradient = jnp.where(preactivation_values > 0, grad_z, 0.0)
-    first_gradient_sum, second_gradient_sum, class_tile = lax.psum(
+    first_gradient_sum, second_gradient_sum, class_tile, loss_tile = lax.psum(
         (
             jnp.sum(preactivation_gradient, 0),
             jnp.sum(preactivation_gradient * normalized_input, 0),
             class_local_slice,
+            jnp.sum(weights_pix * cross),
         ),
         "tile",
     )
-    grad_shift, grad_gain, grad_class = lax.psum(
-        (first_gradient_sum, second_gradient_sum, class_tile), "rep"
+    grad_shift, grad_gain, grad_class, loss_total = butterfly_sum(
+        (first_gradient_sum, second_gradient_sum, class_tile, loss_tile), ("rep",)
     )
+    loss = loss_total / mean_weight / all_pix
     normalized_output_gradient = (
         norm_gain_vector
         * inverse_deviation
@@ -90,30 +124,30 @@
     extended = padded(normalized_output_gradient, (("tile", 1),), RATE)
     extended = jnp.pad(extended, ((0, 0), (0, 0), (RATE, RATE), (0, 0)))
     shifted_list = []
-    for tap_index in range(9):
+    for tap_index in range(taps):
         row_off = RATE - (tap_index // 3 - 1) * RATE
         col_off = RATE - (tap_index % 3 - 1) * RATE
         piece = extended[:, row_off : row_off + tile_rows, col_off : col_off + columns, :]
-        shifted_list.append(piece.reshape(local_pix, out_chans))
-    accum_grad = jnp.zeros((local_pix, in_chans), jnp.float32)
-    for tap_index in range(9):
-        accum_grad = accum_grad + lax.dot_general(
-            shifted_list[tap_index],
-            conv_weight[tap_index],
-            (((1,), (1,)), ((), ())),
-            preferred_element_type=jnp.float32,
-        )
+        shifted_list.append(piece.reshape(local_pix, 1, out_chans))
+    shifted = jnp.concatenate(shifted_list, 1)
+
+    blocks = lax.axis_size("rep") * lax.axis_size("tile")
+    nbits = blocks.bit_length() - 1
+    flat_x = features.reshape((local_pix,) + (2,) * nbits + (in_chans // blocks,))
+    flat_x = flat_x.transpose((0,) + tuple(range(nbits, 0, -1)) + (nbits + 1,))
+    flat_x = flat_x.reshape(local_pix, in_chans)
+    weight_part = lax.dot_general(
+        flat_x, shifted, (((0,), (0,)), ((), ())), preferred_element_type=jnp.float32
+    )
+    grad_weight = halving_scatter(weight_part, ("rep", "tile"))
+
+    accum_grad = lax.dot_general(
+        shifted,
+        conv_weight,
+        (((1, 2), (0, 2)), ((), ())),
+        preferred_element_type=jnp.float32,
+    )
     grad_features = accum_grad.astype(jnp.bfloat16).reshape(images, tile_rows, columns, in_chans)
-    flat_x = features.reshape(local_pix, in_chans)
-    parts_list = [
-        lax.dot_general(
-            flat_x, shifted, (((0,), (0,)), ((), ())), preferred_element_type=jnp.float32
-        )
-        for shifted in shifted_list
-    ]
-    grad_weight = lax.psum_scatter(
-        jnp.stack(parts_list, 1), ("rep", "tile"), scatter_dimension=0, tiled=True
-    )
     return (grad_features, grad_weight, grad_gain, grad_shift, grad_class, loss)
 
 

time: 406 us -> 415 us (1.022)
  local copies, waits for them, and re-layouts: 22.6 us -> 130 us
  matrix products: 116 us -> 40.1 us
  blocking collectives: 82.2 us -> 20.6 us
  starting transfers between devices: 3.01 us -> 40 us
  other arithmetic: 11.1 us -> 25.8 us
  between operations: 16.6 us -> 8.95 us
  waiting for transfers between devices: 154 us -> 147 us
    reduce_scatter x1 -> x0, waiting for transfers between devices: 150 us -> none  [body(): lax.psum_scatter(jnp.stack(parts_list, 1), ('rep', 'tile'), scatter_dimen...]
    ppermute x0 -> x22, waiting for transfers between devices: none -> 147 us  [exchange(): return lax.ppermute(x, axis, pairs)]
    dot_general x9 -> x1, matrix products: 82.6 us -> 18 us  [body(): lax.dot_general(shifted, conv_weight, (((1, 2), (0, 2)), ((), ())), prefe...]
    psum x2 -> x0, blocking collectives: 61.2 us -> none  [the longest x1 39.9 us: body(): lax.psum((jnp.sum(weights_pix), jnp.sum(weights_pix * cross)), ('rep', 't...]
    dynamic_slice x0 -> x3, local copies, waits for them, and re-layouts: none -> 51.3 us  [the longest x2 34.7 us: halving_scatter(): keep = lax.dynamic_index_in_dim(x, mine, 0, keepdims=False)]
    reshape x0 -> x2, local copies, waits for them, and re-layouts: none -> 36.4 us  [the longest x1 19.1 us: body(): features.reshape((local_pix,) + (2,) * nbits + (in_chans // blocks,))]
    ppermute x0 -> x22, starting transfers between devices: none -> 35.5 us  [exchange(): return lax.ppermute(x, axis, pairs)]
    transpose x0 -> x1, local copies, waits for them, and re-layouts: none -> 30.6 us  [body(): flat_x = flat_x.transpose((0,) + tuple(range(nbits, 0, -1)) + (nbits + 1,))]
  transfers between devices with their start and end apart: 3 -> 24, of which waited for: 3 -> 15; matrix products, arithmetic and copies ran while one was open for 21% -> 21% of each run, Pallas kernels for 0% -> 0%
where the time goes in v1:
time: 415 us; the launch traced here: 412 us
  waiting for transfers between devices  147 us (35%)
  local copies, waits for them, and re-layouts  130 us (31%)
  matrix products  40.1 us (10%)
  starting transfers between devices  40 us (10%)
  other arithmetic  25.8 us (6%)
  blocking collectives  20.6 us (5%)
  between operations  8.95 us (2%)
    ppermute x22, waiting for transfers between devices, exchange(): return lax.ppermute(x, axis, pairs)  147 us
    ppermute x22, starting transfers between devices, exchange(): return lax.ppermute(x, axis, pairs)  35.5 us
    dynamic_slice x2, local copies, waits for them, and re-layouts, halving_scatter(): keep = lax.dynamic_index_in_dim(x, mine, 0, keepdims=False)  34.7 us
    transpose x1, local copies, waits for them, and re-layouts, body(): flat_x = flat_x.transpose((0,) + tuple(range(nbits, 0, -1)) + (nbits + 1,))  30.6 us
    reshape x1, local copies, waits for them, and re-layouts, body(): features.reshape((local_pix,) + (2,) * nbits + (in_chans // blocks,))  19.1 us
    dot_general x1, matrix products, body(): lax.dot_general(shifted, conv_weight, (((1, 2), (0, 2)), ((), ())), prefe...  18 us
    reshape x1, local copies, waits for them, and re-layouts, halving_scatter(): x = x.reshape((2, x.shape[0] // 2) + x.shape[1:])  17.3 us
    dynamic_slice x1, local copies, waits for them, and re-layouts, halving_scatter(): send = lax.dynamic_index_in_dim(x, 1 - mine, 0, keepdims=False)  16.6 us
  transfers between devices with their start and end apart: 24, of which 15 were waited for; matrix products, arithmetic and copies ran while one was open for 21% of the time, Pallas kernels for 0%

profile of v1, /device:TPU:0, one launch (start us, length us, event | category | flops | bytes accessed | tf_op | source)
XLA Modules:
  0.0 412.4 jit_solution(12702215151536394408)
XLA Ops:
  2.2 8.4 %psum.42 = f32[256]{0:T(256)S(1)} all-reduce(f32[256]{0:T(256)S(1)} %convert_reduce_fusion), channel_id=1, replica_groups=mesh['rep'=8,'tile'=4] {'tile'}, use_global_device_ids=true, to_apply=%region_1.0 | all-reduce | flops 256 | bytes 2048 | tf_op jit(solution)/shard_map/psum | solution.py:82
  12.0 5.8 %psum.43 = f32[256]{0:T(256)S(1)} all-reduce(f32[256]{0:T(256)S(1)} %multiply_reduce_fusion.1), channel_id=1, replica_groups=mesh['rep'=8,'tile'=4] {'tile'}, use_global_device_ids=true, to_apply=%region_3.0 | all-reduce | flops 256 | bytes 2048 | tf_op jit(solution)/shard_map/psum | solution.py:84
  29.2 2.9 collective-permute-start.2
  33.5 3.0 collective-permute-start.3
  37.7 4.0 collective-permute-start.4
  43.5 3.3 fusion.20
  47.8 6.5 %all-reduce.1 = (f32[256]{0:T(256)S(1)}, f32[256]{0:T(256)S(1)}, f32[3,256]{1,0:T(4,128)S(1)}, f32[]{:T(128)}) all-reduce(f32[256]{0:T(256)S(1)} %get-tuple-element.7, f32[256]{0:T(256)S(1)} %get-tuple-element.6, f32[3,256]{1,0:T(4,128)S(1)} %fusion.7, f32[]{:T(128)} %get-tuple-element.18), channel_id=1, replica_groups=mesh['rep'=8,'tile'=4] {'tile'}, use_global_device_ids=true, to_apply=%region_11.12 | all-reduce | flops 1281 | bytes 10248 | tf_op jit(solution)/shard_map/psum | solution.py:99
  61.1 3.3 collective-permute-start.5
  64.4 19.1 %reshape.116 = bf16[1728,2,2,2,2,2,48]{6,5,4,3,2,1,0:T(2,128)(2,1)} reshape(bf16[2,12,72,1536]{3,2,1,0:T(8,128)(2,1)} %param.8) | data formatting | bytes 10616832 | tf_op jit(solution)/shard_map/reshape | solution.py:136
  83.5 30.6 %copy.27 = bf16[1728,2,2,2,2,2,48]{0,6,1,2,3,4,5:T(8,128)(2,1)} copy(bf16[1728,2,2,2,2,2,48]{6,5,4,3,2,1,0:T(2,128)(2,1)} %reshape.116) | data formatting | bytes 10616832 | tf_op jit(solution)/shard_map/transpose | solution.py:137
  117.2 3.9 copy-done.5
  121.8 16.1 %convolution_bitcast_fusion = f32[1536,9,256]{0,2,1:T(8,128)} fusion(bf16[1728,9,256]{2,0,1:T(8,128)(2,1)S(1)} %constant_dynamic-update-slice_fusion, bf16[1728,1536,1]{0,1,2:T(8,128)(2,1)S(1)} %bitcast.75), kind=kOutput, calls=%fused_computation.5 | convolution fusion | flops 12230590464 | bytes 27426816 | tf_op jit(solution)/shard_map/dot_general | solution.py:139
  137.8 17.3 %reshape.109 = f32[2,768,9,256]{1,0,3,2:T(2,128)} reshape(f32[1536,9,256]{0,2,1:T(8,128)} %convolution_bitcast_fusion) | data formatting | bytes 28311552 | tf_op jit(solution)/shard_map/reshape | solution.py:49
  155.2 18.1 %constant_dynamic-slice_fusion.1 = (f32[1,768,9,256]{1,0,3,2:T(1,128)}, f32[1,768,9,256]{1,0,3,2:T(1,128)}) fusion(f32[2,768,9,256]{1,0,3,2:T(2,128)} %reshape.109, s32[]{:T(128)S(6)} %select_n.40, s32[]{:T(128)S(6)} %select_n.41), kind=kLoop, calls=%fused_computation.56 | loop fusion | bytes 28311560 | tf_op jit(solution)/shard_map/jit(dynamic_index_in_dim)/dynamic_slice | solution.py:50
  173.2 16.6 %copy.24 = f32[1,768,9,256]{3,1,2,0:T(8,128)} copy(f32[1,768,9,256]{1,0,3,2:T(1,128)} %get-tuple-element.21) | data formatting | bytes 14155776 | tf_op jit(solution)/shard_map/jit(dynamic_index_in_dim)/dynamic_slice | solution.py:51
  189.9 16.6 %copy.23 = f32[1,768,9,256]{3,1,2,0:T(8,128)} copy(f32[1,768,9,256]{1,0,3,2:T(1,128)} %get-tuple-element.20) | data formatting | bytes 14155776 | tf_op jit(solution)/shard_map/jit(dynamic_index_in_dim)/dynamic_slice | solution.py:50
  206.5 6.3 %bitcast_add_fusion = f32[768,9,256]{2,0,1:T(8,128)S(1)} fusion(f32[768,9,256]{2,0,1:T(8,128)} %collective-permute-done.7, f32[1,768,9,256]{3,1,2,0:T(8,128)} %copy.23), kind=kLoop, calls=%fused_computation.3 | loop fusion | flops 1769472 | bytes 21233664 | tf_op jit(solution)/shard_map/add | solution.py:52
  215.9 78.9 %collective-permute-done.8 = f32[384,9,256]{2,0,1:T(8,128)} collective-permute-done((f32[384,9,256]{2,0,1:T(8,128)S(1)}, f32[384,9,256]{2,0,1:T(8,128)}, u32[]{:S(2)}, u32[]{:S(2)}) %collective-permute-start.8) | collective-permute-done | bytes 3538976 | tf_op jit(solution)/shard_map/ppermute | solution.py:37
  294.8 3.7 bitcast_add_fusion.1
  301.4 39.0 %collective-permute-done.9 = f32[192,9,256]{2,0,1:T(8,128)} collective-permute-done((f32[192,9,256]{2,0,1:T(8,128)}, f32[192,9,256]{2,0,1:T(8,128)}, u32[]{:S(2)}, u32[]{:S(2)}) %collective-permute-start.9) | collective-permute-done | bytes 1769504 | tf_op jit(solution)/shard_map/ppermute | solution.py:37
  350.8 13.3 %collective-permute-done.19 = f32[3,256]{1,0:T(4,128)S(1)} collective-permute-done((f32[3,256]{1,0:T(4,128)S(1)}, f32[3,256]{1,0:T(4,128)S(1)}, u32[]{:S(2)}, u32[]{:S(2)}) %collective-permute-start.19) | collective-permute-done | bytes 3104 | tf_op jit(solution)/shard_map/ppermute | solution.py:37
  378.2 2.9 collective-permute-start.22
  382.5 2.9 collective-permute-start.23
  392.4 18.0 %bitcast_convert_fusion = bf16[1728,1536]{1,0:T(8,128)(2,1)} fusion(bf16[1728,9,256]{2,0,1:T(8,128)(2,1)} %copy-done.5, bf16[9,1536,256]{2,1,0:T(8,128)(2,1)} %param.10), kind=kOutput, calls=%fused_computation.2 | convolution fusion | flops 12233244672 | bytes 20348928 | tf_op jit(solution)/shard_map/dot_general | solution.py:144
  (103 shorter events, 63.1 us)
Async XLA Ops:
  22.4 1.2 collective-permute-start
  25.0 3.6 collective-permute-start.1
  29.2 3.6 collective-permute-start.2
  33.5 3.6 collective-permute-start.3
  37.7 4.5 %collective-permute-start.4 = (f32[]{:T(128)}, f32[]{:T(128)}, u32[]{:S(2)}, u32[]{:S(2)}) collective-permute-start(f32[]{:T(128)} %add.148), channel_id=1, source_target_pairs={{0,16},{4,20},{8,24},{12,28},{16,0},{20,4},{24,8},{28,12},{1,17},{... | collective-permute-start | bytes 20 | tf_op jit(solution)/shard_map/ppermute | solution.py:37
  54.2 3.6 collective-permute-start.15
  59.8 54.3 %collective-permute-start.6 = (bf16[2,12,72,256]{3,2,1,0:T(8,128)(2,1)S(1)}, bf16[2,12,72,256]{3,2,1,0:T(8,128)(2,1)S(1)}, u32[]{:S(2)}, u32[]{:S(2)}) collective-permute-start(bf16[2,12,72,256]{3,2,1,0:T(8,128)(2,1)S(1)} %bitcast.67), channel_id=1, source_target_pairs={{1,0},{2,1},{3,2},{5,4},{6,5},{7,6},{9,8},{10,9},{11,10},{13,12},{... | collective-permute-start | bytes 2654216 | tf_op jit(solution)/shard_map/ppermute | solution.py:20
  61.1 53.0 %collective-permute-start.5 = (bf16[2,12,72,256]{3,2,1,0:T(8,128)(2,1)S(1)}, bf16[2,12,72,256]{3,2,1,0:T(8,128)(2,1)S(1)}, u32[]{:S(2)}, u32[]{:S(2)}) collective-permute-start(bf16[2,12,72,256]{3,2,1,0:T(8,128)(2,1)S(1)} %bitcast.68), channel_id=1, source_target_pairs={{0,1},{1,2},{2,3},{4,5},{5,6},{6,7},{8,9},{9,10},{10,11},{12,13},{... | collective-permute-start | bytes 2654216 | tf_op jit(solution)/shard_map/ppermute | solution.py:19
  189.9 16.6 %collective-permute-start.7 = (f32[768,9,256]{2,0,1:T(8,128)}, f32[768,9,256]{2,0,1:T(8,128)}, u32[]{:S(2)}, u32[]{:S(2)}) collective-permute-start(f32[768,9,256]{2,0,1:T(8,128)} %bitcast.70), channel_id=1, source_target_pairs={{0,1},{1,0},{2,3},{3,2},{4,5},{5,4},{6,7},{7,6},{8,9},{9,8},{10,11... | collective-permute-start | bytes 21233672 | tf_op jit(solution)/shard_map/ppermute | solution.py:37
  215.7 79.0 %collective-permute-start.8 = (f32[384,9,256]{2,0,1:T(8,128)S(1)}, f32[384,9,256]{2,0,1:T(8,128)}, u32[]{:S(2)}, u32[]{:S(2)}) collective-permute-start(f32[384,9,256]{2,0,1:T(8,128)S(1)} %dynamic-slice_bitcast_fusion), channel_id=1, source_target_pairs={{0,2},{1,3},{2,0},{3,1},{4,6},{5,7},{6,4},{7,5},{8,10},{9,11},{10,... | collective-permute-start | bytes 10616840 | tf_op jit(solution)/shard_map/ppermute | solution.py:37
  299.9 40.6 %collective-permute-start.9 = (f32[192,9,256]{2,0,1:T(8,128)}, f32[192,9,256]{2,0,1:T(8,128)}, u32[]{:S(2)}, u32[]{:S(2)}) collective-permute-start(f32[192,9,256]{2,0,1:T(8,128)} %dynamic-slice_bitcast_fusion.1), channel_id=1, source_target_pairs={{0,4},{4,0},{8,12},{12,8},{16,20},{20,16},{24,28},{28,24},{1,5},{5... | collective-permute-start | bytes 5308424 | tf_op jit(solution)/shard_map/ppermute | solution.py:37
  343.5 45.9 %collective-permute-start.10 = (f32[96,9,256]{2,0,1:T(8,128)S(1)}, f32[96,9,256]{2,0,1:T(8,128)S(1)}, u32[]{:S(2)}, u32[]{:S(2)}) collective-permute-start(f32[96,9,256]{2,0,1:T(8,128)S(1)} %dynamic-slice_bitcast_fusion.2), channel_id=1, source_target_pairs={{0,8},{4,12},{8,0},{12,4},{16,24},{20,28},{24,16},{28,20},{1,9},{5... | collective-permute-start | bytes 2654216 | tf_op jit(solution)/shard_map/ppermute | solution.py:37
  345.2 3.6 collective-permute-start.18
  348.9 15.2 %collective-permute-start.19 = (f32[3,256]{1,0:T(4,128)S(1)}, f32[3,256]{1,0:T(4,128)S(1)}, u32[]{:S(2)}, u32[]{:S(2)}) collective-permute-start(f32[3,256]{1,0:T(4,128)S(1)} %add.172), channel_id=1, source_target_pairs={{0,8},{4,12},{8,0},{12,4},{16,24},{20,28},{24,16},{28,20},{1,9},{5... | collective-permute-start | bytes 9224 | tf_op jit(solution)/shard_map/ppermute | solution.py:37
  349.2 17.5 %collective-permute-start.12 = (f32[256]{0:T(256)S(1)}, f32[256]{0:T(256)S(1)}, u32[]{:S(2)}, u32[]{:S(2)}) collective-permute-start(f32[256]{0:T(256)S(1)} %get-tuple-element.14), channel_id=1, source_target_pairs={{0,4},{4,0},{8,12},{12,8},{16,20},{20,16},{24,28},{28,24},{1,5},{5... | collective-permute-start | bytes 3080 | tf_op jit(solution)/shard_map/ppermute | solution.py:37
  364.1 24.7 %collective-permute-start.20 = (f32[3,256]{1,0:T(4,128)S(1)}, f32[3,256]{1,0:T(4,128)S(1)}, u32[]{:S(2)}, u32[]{:S(2)}) collective-permute-start(f32[3,256]{1,0:T(4,128)S(1)} %add.173), channel_id=1, source_target_pairs={{0,16},{4,20},{8,24},{12,28},{16,0},{20,4},{24,8},{28,12},{1,17},{... | collective-permute-start | bytes 9224 | tf_op jit(solution)/shard_map/ppermute | solution.py:37
  366.7 3.6 collective-permute-start.13
  368.3 3.6 collective-permute-start.16
  370.3 17.3 %collective-permute-start.14 = (f32[256]{0:T(256)S(1)}, f32[256]{0:T(256)S(1)}, u32[]{:S(2)}, u32[]{:S(2)}) collective-permute-start(f32[256]{0:T(256)S(1)} %add.167), channel_id=1, source_target_pairs={{0,16},{4,20},{8,24},{12,28},{16,0},{20,4},{24,8},{28,12},{1,17},{... | collective-permute-start | bytes 3080 | tf_op jit(solution)/shard_map/ppermute | solution.py:37
  371.9 16.3 %collective-permute-start.17 = (f32[256]{0:T(256)S(1)}, f32[256]{0:T(256)S(1)}, u32[]{:S(2)}, u32[]{:S(2)}) collective-permute-start(f32[256]{0:T(256)S(1)} %add.170), channel_id=1, source_target_pairs={{0,16},{4,20},{8,24},{12,28},{16,0},{20,4},{24,8},{28,12},{1,17},{... | collective-permute-start | bytes 3080 | tf_op jit(solution)/shard_map/ppermute | solution.py:37
  373.3 3.6 collective-permute-start.21
  378.2 3.6 collective-permute-start.22
  382.5 4.5 %collective-permute-start.23 = (f32[]{:T(128)}, f32[]{:T(128)}, u32[]{:S(2)}, u32[]{:S(2)}) collective-permute-start(f32[]{:T(128)} %add.176), channel_id=1, source_target_pairs={{0,16},{4,20},{8,24},{12,28},{16,0},{20,4},{24,8},{28,12},{1,17},{... | collective-permute-start | bytes 20 | tf_op jit(solution)/shard_map/ppermute | solution.py:37
  390.8 19.6 %collective-permute-start.11 = (f32[48,9,256]{2,0,1:T(8,128)S(1)}, f32[48,9,256]{2,0,1:T(8,128)S(1)}, u32[]{:S(2)}, u32[]{:S(2)}) collective-permute-start(f32[48,9,256]{2,0,1:T(8,128)S(1)} %dynamic-slice_bitcast_fusion.3), channel_id=1, source_target_pairs={{0,16},{4,20},{8,24},{12,28},{16,0},{20,4},{24,8},{28,12},{1,17},{... | collective-permute-start | bytes 1327112 | tf_op jit(solution)/shard_map/ppermute | solution.py:37
  (12 other events, 175.2 us)

commit v2 on v1

--- a/solution.py
+++ b/solution.py
@@ -43,13 +43,15 @@
     return x
 
 
-def halving_scatter(x, axes):
-    for axis, bit in index_bits(axes):
+def halving_scatter(x, steps, bit_axes):
+    bit_axes = list(bit_axes)
+    for axis, bit, combined in steps:
+        ax = bit_axes.index(combined)
         mine = (lax.axis_index(axis) >> bit) & 1
-        x = x.reshape((2, x.shape[0] // 2) + x.shape[1:])
-        keep = lax.dynamic_index_in_dim(x, mine, 0, keepdims=False)
-        send = lax.dynamic_index_in_dim(x, 1 - mine, 0, keepdims=False)
+        keep = lax.dynamic_index_in_dim(x, mine, ax, keepdims=False)
+        send = lax.dynamic_index_in_dim(x, 1 - mine, ax, keepdims=False)
         x = keep + exchange(send, axis, bit)
+        bit_axes.pop(ax)
     return x
 
 
@@ -76,10 +78,10 @@
         labels.reshape(local_pix, 1) == jnp.arange(classes, dtype=jnp.int32)
     ).astype(jnp.float32)
     weights_pix = jnp.sum(onehot * class_weight.astype(jnp.float32), -1)
-    weight_total = butterfly_sum(jnp.sum(weights_pix), ("rep", "tile"))
 
     yvals = conv_out.astype(jnp.float32).reshape(local_pix, out_chans)
-    column_sum = lax.psum(jnp.sum(yvals, 0), "tile")
+    column_sum, weight_tile = lax.psum((jnp.sum(yvals, 0), jnp.sum(weights_pix)), "tile")
+    weight_total = butterfly_sum(weight_tile, ("rep",))
     centre_offset = yvals - column_sum / per_replica_part
     variance = lax.psum(jnp.sum(centre_offset * centre_offset, 0), "tile") / per_replica_part
     inverse_deviation = lax.rsqrt(variance + 1e-05)
@@ -133,13 +135,13 @@
 
     blocks = lax.axis_size("rep") * lax.axis_size("tile")
     nbits = blocks.bit_length() - 1
-    flat_x = features.reshape((local_pix,) + (2,) * nbits + (in_chans // blocks,))
-    flat_x = flat_x.transpose((0,) + tuple(range(nbits, 0, -1)) + (nbits + 1,))
-    flat_x = flat_x.reshape(local_pix, in_chans)
+    flat_x = features.reshape(local_pix, in_chans)
     weight_part = lax.dot_general(
         flat_x, shifted, (((0,), (0,)), ((), ())), preferred_element_type=jnp.float32
     )
-    grad_weight = halving_scatter(weight_part, ("rep", "tile"))
+    weight_part = weight_part.reshape((2,) * nbits + (in_chans // blocks, taps, out_chans))
+    bits = [(axis, bit, combined) for combined, (axis, bit) in enumerate(index_bits(("rep", "tile")))]
+    bit_axes = list(range(nbits - 1, -1, -1))
 
     accum_grad = lax.dot_general(
         shifted,
@@ -147,6 +149,24 @@
         (((1, 2), (0, 2)), ((), ())),
         preferred_element_type=jnp.float32,
     )
+    axis, bit, combined = bits[0]
+    ax = bit_axes.index(combined)
+    mine = (lax.axis_index(axis) >> bit) & 1
+    keep = lax.dynamic_index_in_dim(weight_part, mine, ax, keepdims=False)
+    send = lax.dynamic_index_in_dim(weight_part, 1 - mine, ax, keepdims=False)
+    received, accum_grad = lax.optimization_barrier((exchange(send, axis, bit), accum_grad))
+    half = keep + received
+    bit_axes.pop(ax)
+    rest = bits[1:]
+    streams = 3
+    per = taps // streams
+    pieces = []
+    for s in range(streams):
+        order = rest[s:] + rest[:s]
+        chunk = lax.slice_in_dim(half, s * per, (s + 1) * per if s < streams - 1 else taps, axis=half.ndim - 2)
+        pieces.append(halving_scatter(chunk, order, bit_axes))
+    grad_weight = jnp.concatenate(pieces, 1)
+
     grad_features = accum_grad.astype(jnp.bfloat16).reshape(images, tile_rows, columns, in_chans)
     return (grad_features, grad_weight, grad_gain, grad_shift, grad_class, loss)
 

time: 415 us -> 286 us (0.69)
  local copies, waits for them, and re-layouts: 130 us -> 52.3 us
  waiting for transfers between devices: 147 us -> 72 us
  starting transfers between devices: 40 us -> 59.4 us
  blocking collectives: 20.6 us -> 26.9 us
    ppermute x22 -> x28, waiting for transfers between devices: 147 us -> 70.2 us  [exchange(): return lax.ppermute(x, axis, pairs)]
    reshape x2 -> x0, local copies, waits for them, and re-layouts: 36.4 us -> none  [the longest x1 19.1 us: body(): features.reshape((local_pix,) + (2,) * nbits + (in_chans // blocks,))]
    dynamic_slice x3 -> x2, local copies, waits for them, and re-layouts: 51.3 us -> 19.7 us  [the longest x1 13 us: body(): keep = lax.dynamic_index_in_dim(weight_part, mine, ax, keepdims=False)]
    transpose x1 -> x0, local copies, waits for them, and re-layouts: 30.6 us -> none  [body(): flat_x = flat_x.transpose((0,) + tuple(range(nbits, 0, -1)) + (nbits + 1,))]
    ppermute x22 -> x28, starting transfers between devices: 35.5 us -> 54.9 us  [exchange(): return lax.ppermute(x, axis, pairs)]
    dot_general x0 -> x1, local copies, waits for them, and re-layouts: none -> 15.1 us  [body(): lax.dot_general(flat_x, shifted, (((0,), (0,)), ((), ())), preferred_elem...]
    add x5 -> x12, other arithmetic: 13.9 us -> 5.28 us  [halving_scatter(): x = keep + exchange(send, axis, bit)]
    add x0 -> x1, other arithmetic: none -> 7.71 us  [body(): half = keep + received]
  transfers between devices with their start and end apart: 24 -> 30, of which waited for: 15 -> 19; matrix products, arithmetic and copies ran while one was open for 21% -> 11% of each run, Pallas kernels for 0% -> 0%
where the time goes in v2:
time: 286 us; the launch traced here: 285 us
  waiting for transfers between devices  72 us (25%)
  starting transfers between devices  59.4 us (21%)
  local copies, waits for them, and re-layouts  52.3 us (18%)
  matrix products  40.2 us (14%)
  other arithmetic  27.2 us (10%)
  blocking collectives  26.9 us (9%)
  between operations  7.45 us (3%)
    ppermute x28, waiting for transfers between devices, exchange(): return lax.ppermute(x, axis, pairs)  70.2 us
    ppermute x28, starting transfers between devices, exchange(): return lax.ppermute(x, axis, pairs)  54.9 us
    dot_general x1, matrix products, body(): lax.dot_general(shifted, conv_weight, (((1, 2), (0, 2)), ((), ())), prefe...  18.1 us
    dot_general x1, matrix products, body(): lax.dot_general(flat_x, shifted, (((0,), (0,)), ((), ())), preferred_elem...  16.1 us
    dot_general x1, local copies, waits for them, and re-layouts, body(): lax.dot_general(flat_x, shifted, (((0,), (0,)), ((), ())), preferred_elem...  15.1 us
    psum x2, blocking collectives, body(): lax.psum((jnp.sum(yvals, 0), jnp.sum(weights_pix)), 'tile')  14.7 us
    dynamic_slice x1, local copies, waits for them, and re-layouts, body(): keep = lax.dynamic_index_in_dim(weight_part, mine, ax, keepdims=False)  13 us
    add x1, other arithmetic, body(): half = keep + received  7.71 us
  transfers between devices with their start and end apart: 30, of which 19 were waited for; matrix products, arithmetic and copies ran while one was open for 11% of the time, Pallas kernels for 0%

profile of v2, /device:TPU:0, one launch (start us, length us, event | category | flops | bytes accessed | tf_op | source)
XLA Modules:
  0.0 285.4 jit_solution(12791415200188763169)
XLA Ops:
  2.8 8.4 %psum.49 = f32[256]{0:T(256)S(1)} all-reduce(f32[256]{0:T(256)S(1)} %convert_reduce_fusion), channel_id=1, replica_groups=mesh['rep'=8,'tile'=4] {'tile'}, use_global_device_ids=true, to_apply=%region_1.0 | all-reduce | flops 256 | bytes 2048 | tf_op jit(solution)/shard_map/psum | solution.py:83
  12.7 5.8 %psum.50 = f32[256]{0:T(256)S(1)} all-reduce(f32[256]{0:T(256)S(1)} %multiply_reduce_fusion.1), channel_id=1, replica_groups=mesh['rep'=8,'tile'=4] {'tile'}, use_global_device_ids=true, to_apply=%region_3.0 | all-reduce | flops 256 | bytes 2048 | tf_op jit(solution)/shard_map/psum | solution.py:86
  22.6 6.4 %psum.51 = f32[]{:T(128)} all-reduce(f32[]{:T(128)} %get-tuple-element.17), channel_id=1, replica_groups=mesh['rep'=8,'tile'=4] {'tile'}, use_global_device_ids=true, to_apply=%region_6.0 | all-reduce | flops 1 | bytes 8 | tf_op jit(solution)/shard_map/psum | solution.py:83
  38.3 4.0 %collective-permute-start.2 = (f32[]{:T(128)}, f32[]{:T(128)}, u32[]{:S(2)}, u32[]{:S(2)}) collective-permute-start(f32[]{:T(128)} %add.187), channel_id=1, source_target_pairs={{0,16},{4,20},{8,24},{12,28},{16,0},{20,4},{24,8},{28,12},{1,17},{... | collective-permute-start | bytes 20 | tf_op jit(solution)/shard_map/ppermute | solution.py:37
  45.2 3.3 %fusion.20 = (f32[256]{0:T(256)S(1)}, f32[256]{0:T(256)S(1)}, f32[1728,256]{1,0:T(8,128)}) fusion(f32[256]{0:T(256)S(1)} %get-tuple-element.39, f32[256]{0:T(256)S(1)} %broadcast_multiply_fusion.1, bf16[2,12,72,256]{3,2,1,0:T(8,128)(2,1)S(1)} %copy-done.2, f32[3,256]{1,0:T(4,128)S(1)} %copy-done, f32[1728,3]{0,1:T(4,128)S(1)} %get-tuple-element.41, ...), kind=kOutput, calls=%fused_computation.81 | convolution fusion | flops 20374336 | bytes 4474368 | tf_op jit(solution)/shard_map/dot_general | solution.py:99
  48.5 6.4 %all-reduce.1 = (f32[256]{0:T(256)S(1)}, f32[256]{0:T(256)S(1)}, f32[3,256]{1,0:T(4,128)S(1)}, f32[]{:T(128)}) all-reduce(f32[256]{0:T(256)S(1)} %get-tuple-element.11, f32[256]{0:T(256)S(1)} %get-tuple-element.10, f32[3,256]{1,0:T(4,128)S(1)} %fusion.7, f32[]{:T(128)} %get-tuple-element.22), channel_id=1, replica_groups=mesh['rep'=8,'tile'=4] {'tile'}, use_global_device_ids=true, to_apply=%region_12.13 | all-reduce | flops 1281 | bytes 10248 | tf_op jit(solution)/shard_map/psum | solution.py:101
  61.8 3.3 %collective-permute-start.3 = (bf16[2,12,72,256]{3,2,1,0:T(8,128)(2,1)S(1)}, bf16[2,12,72,256]{3,2,1,0:T(8,128)(2,1)S(1)}, u32[]{:S(2)}, u32[]{:S(2)}) collective-permute-start(bf16[2,12,72,256]{3,2,1,0:T(8,128)(2,1)S(1)} %bitcast.91), channel_id=1, source_target_pairs={{0,1},{1,2},{2,3},{4,5},{5,6},{6,7},{8,9},{9,10},{10,11},{12,13},{... | collective-permute-start | bytes 2654216 | tf_op jit(solution)/shard_map/ppermute | solution.py:19
  69.9 3.8 %copy-done.5 = bf16[1728,9,256]{2,0,1:T(8,128)(2,1)} copy-done((bf16[1728,9,256]{2,0,1:T(8,128)(2,1)}, bf16[1728,9,256]{2,0,1:T(8,128)(2,1)S(1)}, u32[]{:S(2)}) %copy-start.5) | copy-done | bytes 7962648
  74.3 16.1 %convolution_bitcast_fusion.1 = f32[1536,9,256]{0,2,1:T(8,128)} fusion(bf16[1728,9,256]{2,0,1:T(8,128)(2,1)S(1)} %constant_dynamic-update-slice_fusion, bf16[1728,1536,1]{1,0,2:T(8,128)(2,1)S(1)} %bitcast.103), kind=kOutput, calls=%fused_computation.6 | convolution fusion | flops 12230590464 | bytes 27426816 | tf_op jit(solution)/shard_map/dot_general | solution.py:139
  90.3 15.1 %copy.17 = f32[1536,9,256]{2,0,1:T(8,128)} copy(f32[1536,9,256]{0,2,1:T(8,128)} %convolution_bitcast_fusion.1) | data formatting | bytes 28311552 | tf_op jit(solution)/shard_map/dot_general | solution.py:139
  105.5 13.0 %constant_dynamic-slice_fusion = (f32[2,2,2,2,1,48,9,256]{7,5,4,3,2,1,0,6:T(8,128)}, f32[2,2,2,2,1,48,9,256]{7,5,4,3,2,1,0,6:T(8,128)}) fusion(f32[2,2,2,2,2,48,9,256]{7,5,4,3,2,1,0,6:T(8,128)} %bitcast.87, s32[]{:T(128)S(6)} %select_n.62, s32[]{:T(128)S(6)} %select_n.61), kind=kLoop, calls=%fused_computation.72 | loop fusion | bytes 28311560 | tf_op jit(solution)/shard_map/jit(dynamic_index_in_dim)/dynamic_slice | solution.py:155
  118.4 6.7 %copy.22 = f32[2,2,2,2,1,48,9,256]{7,5,6,4,3,2,1,0:T(8,128)} copy(f32[2,2,2,2,1,48,9,256]{7,5,4,3,2,1,0,6:T(8,128)} %get-tuple-element.25) | data formatting | bytes 14155776 | tf_op jit(solution)/shard_map/jit(dynamic_index_in_dim)/dynamic_slice | solution.py:156
  125.1 8.9 %collective-permute-start.5 = (f32[2,2,2,2,48,9,256]{6,4,5,3,2,1,0:T(8,128)}, f32[2,2,2,2,48,9,256]{6,4,5,3,2,1,0:T(8,128)}, u32[]{:S(2)}, u32[]{:S(2)}) collective-permute-start(f32[2,2,2,2,48,9,256]{6,4,5,3,2,1,0:T(8,128)} %bitcast.86), channel_id=1, source_target_pairs={{0,1},{1,0},{2,3},{3,2},{4,5},{5,4},{6,7},{7,6},{8,9},{9,8},{10,11... | collective-permute-start | bytes 21233672 | tf_op jit(solution)/shard_map/ppermute | solution.py:37
  134.0 18.1 %convolution_bitcast_fusion = bf16[1728,1536]{1,0:T(8,128)(2,1)} fusion(bf16[1728,9,256]{2,0,1:T(8,128)(2,1)} %copy-done.5, bf16[9,1536,256]{2,1,0:T(8,128)(2,1)} %param.10), kind=kOutput, calls=%fused_computation.2 | convolution fusion | flops 12230590464 | bytes 20348928 | tf_op jit(solution)/shard_map/dot_general | solution.py:146
  152.1 7.7 %bitcast_add_fusion = f32[2,2,2,2,48,9,256]{6,4,5,3,2,1,0:T(8,128)} fusion(f32[2,2,2,2,48,9,256]{6,4,5,3,2,1,0:T(8,128)} %collective-permute-done.5, f32[2,2,2,2,1,48,9,256]{7,5,4,3,2,1,0,6:T(8,128)S(1)} %bitcast.89), kind=kLoop, calls=%fused_computation.3 | loop fusion | flops 1769472 | bytes 21233664 | tf_op jit(solution)/shard_map/add | solution.py:158
  159.8 5.3 %fusion.21 = (f32[2,2,2,2,48,3,256]{6,4,5,3,2,1,0:T(8,128)S(1)}, f32[2,2,2,2,48,3,256]{6,4,5,3,2,1,0:T(8,128)}, f32[2,2,2,2,48,3,256]{6,4,5,3,2,1,0:T(8,128)S(1)}) fusion(f32[2,2,2,2,48,9,256]{6,4,5,3,2,1,0:T(8,128)} %bitcast_add_fusion), kind=kLoop, calls=%fused_computation.82 | loop fusion | bytes 14155776 | tf_op jit(solution)/shard_map/slice | solution.py:166
  176.2 18.5 %collective-permute-done.24 = f32[3,256]{1,0:T(4,128)S(1)} collective-permute-done((f32[3,256]{1,0:T(4,128)S(1)}, f32[3,256]{1,0:T(4,128)S(1)}, u32[]{:S(2)}, u32[]{:S(2)}) %collective-permute-start.24) | collective-permute-done | bytes 3104 | tf_op jit(solution)/shard_map/ppermute | solution.py:37
  205.7 3.9 %collective-permute-start.29 = (f32[]{:T(128)}, f32[]{:T(128)}, u32[]{:S(2)}, u32[]{:S(2)}) collective-permute-start(f32[]{:T(128)} %add.223), channel_id=1, source_target_pairs={{0,16},{4,20},{8,24},{12,28},{16,0},{20,4},{24,8},{28,12},{1,17},{... | collective-permute-start | bytes 20 | tf_op jit(solution)/shard_map/ppermute | solution.py:37
  221.7 3.2 %collective-permute-done.23 = f32[256]{0:T(256)} collective-permute-done((f32[256]{0:T(256)S(1)}, f32[256]{0:T(256)}, u32[]{:S(2)}, u32[]{:S(2)}) %collective-permute-start.23) | collective-permute-done | bytes 1056 | tf_op jit(solution)/shard_map/ppermute | solution.py:37
  240.2 12.4 %collective-permute-done.11 = f32[2,2,48,3,256]{4,2,3,1,0:T(8,128)S(1)} collective-permute-done((f32[2,2,48,3,256]{4,2,3,1,0:T(8,128)S(1)}, f32[2,2,48,3,256]{4,2,3,1,0:T(8,128)S(1)}, u32[]{:S(2)}, u32[]{:S(2)}) %collective-permute-start.11) | collective-permute-done | bytes 589856 | tf_op jit(solution)/shard_map/ppermute | solution.py:37
  252.8 12.1 %collective-permute-done.15 = f32[2,2,48,3,256]{4,2,3,1,0:T(8,128)S(1)} collective-permute-done((f32[2,2,48,3,256]{4,2,3,1,0:T(8,128)S(1)}, f32[2,2,48,3,256]{4,2,3,1,0:T(8,128)S(1)}, u32[]{:S(2)}, u32[]{:S(2)}) %collective-permute-start.15) | collective-permute-done | bytes 589856 | tf_op jit(solution)/shard_map/ppermute | solution.py:37
  265.0 3.2 %collective-permute-start.16 = (f32[2,48,3,256]{3,1,2,0:T(8,128)S(1)}, f32[2,48,3,256]{3,1,2,0:T(8,128)S(1)}, u32[]{:S(2)}, u32[]{:S(2)}) collective-permute-start(f32[2,48,3,256]{3,1,2,0:T(8,128)S(1)} %dynamic-slice_bitcast_fusion.6), channel_id=1, source_target_pairs={{0,2},{1,3},{2,0},{3,1},{4,6},{5,7},{6,4},{7,5},{8,10},{9,11},{10,... | collective-permute-start | bytes 884744 | tf_op jit(solution)/shard_map/ppermute | solution.py:37
  268.5 3.9 %collective-permute-start.13 = (f32[48,3,256]{2,0,1:T(8,128)S(1)}, f32[48,3,256]{2,0,1:T(8,128)S(1)}, u32[]{:S(2)}, u32[]{:S(2)}) collective-permute-start(f32[48,3,256]{2,0,1:T(8,128)S(1)} %dynamic-slice_bitcast_fusion.10), channel_id=1, source_target_pairs={{0,2},{1,3},{2,0},{3,1},{4,6},{5,7},{6,4},{7,5},{8,10},{9,11},{10,... | collective-permute-start | bytes 442376 | tf_op jit(solution)/shard_map/ppermute | solution.py:37
  278.7 4.7 %collective-permute-done.9 = f32[48,3,256]{2,0,1:T(8,128)S(1)} collective-permute-done((f32[48,3,256]{2,0,1:T(8,128)S(1)}, f32[48,3,256]{2,0,1:T(8,128)S(1)}, u32[]{:S(2)}, u32[]{:S(2)}) %collective-permute-start.9) | collective-permute-done | bytes 147488 | tf_op jit(solution)/shard_map/ppermute | solution.py:37
  (136 shorter events, 83.9 us)
Async XLA Ops:
  28.9 3.8 %collective-permute-start = (f32[]{:T(128)}, f32[]{:T(128)}, u32[]{:S(2)}, u32[]{:S(2)}) collective-permute-start(f32[]{:T(128)} %psum.51), channel_id=1, source_target_pairs={{0,4},{4,0},{8,12},{12,8},{16,20},{20,16},{24,28},{28,24},{1,5},{5... | collective-permute-start | bytes 20 | tf_op jit(solution)/shard_map/ppermute | solution.py:37
  38.3 4.6 %collective-permute-start.2 = (f32[]{:T(128)}, f32[]{:T(128)}, u32[]{:S(2)}, u32[]{:S(2)}) collective-permute-start(f32[]{:T(128)} %add.187), channel_id=1, source_target_pairs={{0,16},{4,20},{8,24},{12,28},{16,0},{20,4},{24,8},{28,12},{1,17},{... | collective-permute-start | bytes 20 | tf_op jit(solution)/shard_map/ppermute | solution.py:37
  60.5 4.6 %collective-permute-start.4 = (bf16[2,12,72,256]{3,2,1,0:T(8,128)(2,1)S(1)}, bf16[2,12,72,256]{3,2,1,0:T(8,128)(2,1)S(1)}, u32[]{:S(2)}, u32[]{:S(2)}) collective-permute-start(bf16[2,12,72,256]{3,2,1,0:T(8,128)(2,1)S(1)} %bitcast.90), channel_id=1, source_target_pairs={{1,0},{2,1},{3,2},{5,4},{6,5},{7,6},{9,8},{10,9},{11,10},{13,12},{... | collective-permute-start | bytes 2654216 | tf_op jit(solution)/shard_map/ppermute | solution.py:20
  61.8 5.1 %collective-permute-start.3 = (bf16[2,12,72,256]{3,2,1,0:T(8,128)(2,1)S(1)}, bf16[2,12,72,256]{3,2,1,0:T(8,128)(2,1)S(1)}, u32[]{:S(2)}, u32[]{:S(2)}) collective-permute-start(bf16[2,12,72,256]{3,2,1,0:T(8,128)(2,1)S(1)} %bitcast.91), channel_id=1, source_target_pairs={{0,1},{1,2},{2,3},{4,5},{5,6},{6,7},{8,9},{9,10},{10,11},{12,13},{... | collective-permute-start | bytes 2654216 | tf_op jit(solution)/shard_map/ppermute | solution.py:19
  125.1 27.0 %collective-permute-start.5 = (f32[2,2,2,2,48,9,256]{6,4,5,3,2,1,0:T(8,128)}, f32[2,2,2,2,48,9,256]{6,4,5,3,2,1,0:T(8,128)}, u32[]{:S(2)}, u32[]{:S(2)}) collective-permute-start(f32[2,2,2,2,48,9,256]{6,4,5,3,2,1,0:T(8,128)} %bitcast.86), channel_id=1, source_target_pairs={{0,1},{1,0},{2,3},{3,2},{4,5},{5,4},{6,7},{7,6},{8,9},{9,8},{10,11... | collective-permute-start | bytes 21233672 | tf_op jit(solution)/shard_map/ppermute | solution.py:37
  166.6 64.7 %collective-permute-start.10 = (f32[2,2,2,48,3,256]{5,3,4,2,1,0:T(8,128)S(1)}, f32[2,2,2,48,3,256]{5,3,4,2,1,0:T(8,128)}, u32[]{:S(2)}, u32[]{:S(2)}) collective-permute-start(f32[2,2,2,48,3,256]{5,3,4,2,1,0:T(8,128)S(1)} %dynamic-slice_bitcast_fusion.1), channel_id=1, source_target_pairs={{0,4},{4,0},{8,12},{12,8},{16,20},{20,16},{24,28},{28,24},{1,5},{5... | collective-permute-start | bytes 3538952 | tf_op jit(solution)/shard_map/ppermute | solution.py:37
  170.6 63.3 %collective-permute-start.14 = (f32[2,2,2,48,3,256]{5,3,4,2,1,0:T(8,128)}, f32[2,2,2,48,3,256]{5,3,4,2,1,0:T(8,128)}, u32[]{:S(2)}, u32[]{:S(2)}) collective-permute-start(f32[2,2,2,48,3,256]{5,3,4,2,1,0:T(8,128)} %dynamic-slice_bitcast_fusion), channel_id=1, source_target_pairs={{0,8},{4,12},{8,0},{12,4},{16,24},{20,28},{24,16},{28,20},{1,9},{5... | collective-permute-start | bytes 3538952 | tf_op jit(solution)/shard_map/ppermute | solution.py:37
  173.3 63.8 %collective-permute-start.6 = (f32[2,2,2,48,3,256]{5,3,4,2,1,0:T(8,128)}, f32[2,2,2,48,3,256]{5,3,4,2,1,0:T(8,128)}, u32[]{:S(2)}, u32[]{:S(2)}) collective-permute-start(f32[2,2,2,48,3,256]{5,3,4,2,1,0:T(8,128)} %dynamic-slice_bitcast_fusion.2), channel_id=1, source_target_pairs={{0,2},{1,3},{2,0},{3,1},{4,6},{5,7},{6,4},{7,5},{8,10},{9,11},{10,... | collective-permute-start | bytes 3538952 | tf_op jit(solution)/shard_map/ppermute | solution.py:37
  175.7 19.0 %collective-permute-start.24 = (f32[3,256]{1,0:T(4,128)S(1)}, f32[3,256]{1,0:T(4,128)S(1)}, u32[]{:S(2)}, u32[]{:S(2)}) collective-permute-start(f32[3,256]{1,0:T(4,128)S(1)} %get-tuple-element.20), channel_id=1, source_target_pairs={{0,4},{4,0},{8,12},{12,8},{16,20},{20,16},{24,28},{28,24},{1,5},{5... | collective-permute-start | bytes 9224 | tf_op jit(solution)/shard_map/ppermute | solution.py:37
  194.7 19.5 %collective-permute-start.25 = (f32[3,256]{1,0:T(4,128)S(1)}, f32[3,256]{1,0:T(4,128)S(1)}, u32[]{:S(2)}, u32[]{:S(2)}) collective-permute-start(f32[3,256]{1,0:T(4,128)S(1)} %add.219), channel_id=1, source_target_pairs={{0,8},{4,12},{8,0},{12,4},{16,24},{20,28},{24,16},{28,20},{1,9},{5... | collective-permute-start | bytes 9224 | tf_op jit(solution)/shard_map/ppermute | solution.py:37
  205.7 4.5 %collective-permute-start.29 = (f32[]{:T(128)}, f32[]{:T(128)}, u32[]{:S(2)}, u32[]{:S(2)}) collective-permute-start(f32[]{:T(128)} %add.223), channel_id=1, source_target_pairs={{0,16},{4,20},{8,24},{12,28},{16,0},{20,4},{24,8},{28,12},{1,17},{... | collective-permute-start | bytes 20 | tf_op jit(solution)/shard_map/ppermute | solution.py:37
  214.2 5.7 %collective-permute-start.19 = (f32[256]{0:T(256)S(1)}, f32[256]{0:T(256)S(1)}, u32[]{:S(2)}, u32[]{:S(2)}) collective-permute-start(f32[256]{0:T(256)S(1)} %add.213), channel_id=1, source_target_pairs={{0,8},{4,12},{8,0},{12,4},{16,24},{20,28},{24,16},{28,20},{1,9},{5... | collective-permute-start | bytes 3080 | tf_op jit(solution)/shard_map/ppermute | solution.py:37
  217.3 13.4 %collective-permute-start.26 = (f32[3,256]{1,0:T(4,128)S(1)}, f32[3,256]{1,0:T(4,128)S(1)}, u32[]{:S(2)}, u32[]{:S(2)}) collective-permute-start(f32[3,256]{1,0:T(4,128)S(1)} %add.220), channel_id=1, source_target_pairs={{0,16},{4,20},{8,24},{12,28},{16,0},{20,4},{24,8},{28,12},{1,17},{... | collective-permute-start | bytes 9224 | tf_op jit(solution)/shard_map/ppermute | solution.py:37
  220.5 4.4 %collective-permute-start.23 = (f32[256]{0:T(256)S(1)}, f32[256]{0:T(256)}, u32[]{:S(2)}, u32[]{:S(2)}) collective-permute-start(f32[256]{0:T(256)S(1)} %add.217), channel_id=1, source_target_pairs={{0,16},{4,20},{8,24},{12,28},{16,0},{20,4},{24,8},{28,12},{1,17},{... | collective-permute-start | bytes 3080 | tf_op jit(solution)/shard_map/ppermute | solution.py:37
  224.9 4.6 %collective-permute-start.20 = (f32[256]{0:T(256)S(1)}, f32[256]{0:T(256)}, u32[]{:S(2)}, u32[]{:S(2)}) collective-permute-start(f32[256]{0:T(256)S(1)} %add.214), channel_id=1, source_target_pairs={{0,16},{4,20},{8,24},{12,28},{16,0},{20,4},{24,8},{28,12},{1,17},{... | collective-permute-start | bytes 3080 | tf_op jit(solution)/shard_map/ppermute | solution.py:37
  233.3 19.3 %collective-permute-start.11 = (f32[2,2,48,3,256]{4,2,3,1,0:T(8,128)S(1)}, f32[2,2,48,3,256]{4,2,3,1,0:T(8,128)S(1)}, u32[]{:S(2)}, u32[]{:S(2)}) collective-permute-start(f32[2,2,48,3,256]{4,2,3,1,0:T(8,128)S(1)} %dynamic-slice_bitcast_fusion.4), channel_id=1, source_target_pairs={{0,8},{4,12},{8,0},{12,4},{16,24},{20,28},{24,16},{28,20},{1,9},{5... | collective-permute-start | bytes 1769480 | tf_op jit(solution)/shard_map/ppermute | solution.py:37
  235.4 29.5 %collective-permute-start.15 = (f32[2,2,48,3,256]{4,2,3,1,0:T(8,128)S(1)}, f32[2,2,48,3,256]{4,2,3,1,0:T(8,128)S(1)}, u32[]{:S(2)}, u32[]{:S(2)}) collective-permute-start(f32[2,2,48,3,256]{4,2,3,1,0:T(8,128)S(1)} %dynamic-slice_bitcast_fusion.3), channel_id=1, source_target_pairs={{0,16},{4,20},{8,24},{12,28},{16,0},{20,4},{24,8},{28,12},{1,17},{... | collective-permute-start | bytes 1769480 | tf_op jit(solution)/shard_map/ppermute | solution.py:37
  238.6 29.6 %collective-permute-start.7 = (f32[2,2,48,3,256]{4,2,3,1,0:T(8,128)S(1)}, f32[2,2,48,3,256]{4,2,3,1,0:T(8,128)S(1)}, u32[]{:S(2)}, u32[]{:S(2)}) collective-permute-start(f32[2,2,48,3,256]{4,2,3,1,0:T(8,128)S(1)} %dynamic-slice_bitcast_fusion.5), channel_id=1, source_target_pairs={{0,4},{4,0},{8,12},{12,8},{16,20},{20,16},{24,28},{28,24},{1,5},{5... | collective-permute-start | bytes 1769480 | tf_op jit(solution)/shard_map/ppermute | solution.py:37
  252.7 15.7 %collective-permute-start.12 = (f32[2,48,3,256]{3,1,2,0:T(8,128)S(1)}, f32[2,48,3,256]{3,1,2,0:T(8,128)S(1)}, u32[]{:S(2)}, u32[]{:S(2)}) collective-permute-start(f32[2,48,3,256]{3,1,2,0:T(8,128)S(1)} %dynamic-slice_bitcast_fusion.7), channel_id=1, source_target_pairs={{0,16},{4,20},{8,24},{12,28},{16,0},{20,4},{24,8},{28,12},{1,17},{... | collective-permute-start | bytes 884744 | tf_op jit(solution)/shard_map/ppermute | solution.py:37
  265.0 7.9 %collective-permute-start.16 = (f32[2,48,3,256]{3,1,2,0:T(8,128)S(1)}, f32[2,48,3,256]{3,1,2,0:T(8,128)S(1)}, u32[]{:S(2)}, u32[]{:S(2)}) collective-permute-start(f32[2,48,3,256]{3,1,2,0:T(8,128)S(1)} %dynamic-slice_bitcast_fusion.6), channel_id=1, source_target_pairs={{0,2},{1,3},{2,0},{3,1},{4,6},{5,7},{6,4},{7,5},{8,10},{9,11},{10,... | collective-permute-start | bytes 884744 | tf_op jit(solution)/shard_map/ppermute | solution.py:37
  268.3 8.4 %collective-permute-start.8 = (f32[2,48,3,256]{3,1,2,0:T(8,128)S(1)}, f32[2,48,3,256]{3,1,2,0:T(8,128)S(1)}, u32[]{:S(2)}, u32[]{:S(2)}) collective-permute-start(f32[2,48,3,256]{3,1,2,0:T(8,128)S(1)} %dynamic-slice_bitcast_fusion.8), channel_id=1, source_target_pairs={{0,8},{4,12},{8,0},{12,4},{16,24},{20,28},{24,16},{28,20},{1,9},{5... | collective-permute-start | bytes 884744 | tf_op jit(solution)/shard_map/ppermute | solution.py:37
  268.5 8.3 %collective-permute-start.13 = (f32[48,3,256]{2,0,1:T(8,128)S(1)}, f32[48,3,256]{2,0,1:T(8,128)S(1)}, u32[]{:S(2)}, u32[]{:S(2)}) collective-permute-start(f32[48,3,256]{2,0,1:T(8,128)S(1)} %dynamic-slice_bitcast_fusion.10), channel_id=1, source_target_pairs={{0,2},{1,3},{2,0},{3,1},{4,6},{5,7},{6,4},{7,5},{8,10},{9,11},{10,... | collective-permute-start | bytes 442376 | tf_op jit(solution)/shard_map/ppermute | solution.py:37
  273.0 5.7 %collective-permute-start.17 = (f32[48,3,256]{2,0,1:T(8,128)S(1)}, f32[48,3,256]{2,0,1:T(8,128)S(1)}, u32[]{:S(2)}, u32[]{:S(2)}) collective-permute-start(f32[48,3,256]{2,0,1:T(8,128)S(1)} %dynamic-slice_bitcast_fusion.9), channel_id=1, source_target_pairs={{0,4},{4,0},{8,12},{12,8},{16,20},{20,16},{24,28},{28,24},{1,5},{5... | collective-permute-start | bytes 442376 | tf_op jit(solution)/shard_map/ppermute | solution.py:37
  276.8 6.7 %collective-permute-start.9 = (f32[48,3,256]{2,0,1:T(8,128)S(1)}, f32[48,3,256]{2,0,1:T(8,128)S(1)}, u32[]{:S(2)}, u32[]{:S(2)}) collective-permute-start(f32[48,3,256]{2,0,1:T(8,128)S(1)} %dynamic-slice_bitcast_fusion.11), channel_id=1, source_target_pairs={{0,16},{4,20},{8,24},{12,28},{16,0},{20,4},{24,8},{28,12},{1,17},{... | collective-permute-start | bytes 442376 | tf_op jit(solution)/shard_map/ppermute | solution.py:37
  (20 other events, 174.7 us)

commit v3 on v2

--- a/solution.py
+++ b/solution.py
@@ -80,7 +80,8 @@
     weights_pix = jnp.sum(onehot * class_weight.astype(jnp.float32), -1)
 
     yvals = conv_out.astype(jnp.float32).reshape(local_pix, out_chans)
-    column_sum, weight_tile = lax.psum((jnp.sum(yvals, 0), jnp.sum(weights_pix)), "tile")
+    first_sums = lax.psum(jnp.concatenate([jnp.sum(yvals, 0), jnp.sum(weights_pix)[None]]), "tile")
+    column_sum, weight_tile = first_sums[:out_chans], first_sums[out_chans]
     weight_total = butterfly_sum(weight_tile, ("rep",))
     centre_offset = yvals - column_sum / per_replica_part
     variance = lax.psum(jnp.sum(centre_offset * centre_offset, 0), "tile") / per_replica_part
@@ -130,42 +131,46 @@
         row_off = RATE - (tap_index // 3 - 1) * RATE
         col_off = RATE - (tap_index % 3 - 1) * RATE
         piece = extended[:, row_off : row_off + tile_rows, col_off : col_off + columns, :]
-        shifted_list.append(piece.reshape(local_pix, 1, out_chans))
+        shifted_list.append(piece.reshape(local_pix, out_chans))
     shifted = jnp.concatenate(shifted_list, 1)
 
     blocks = lax.axis_size("rep") * lax.axis_size("tile")
     nbits = blocks.bit_length() - 1
+    rows = in_chans // blocks
     flat_x = features.reshape(local_pix, in_chans)
-    weight_part = lax.dot_general(
-        flat_x, shifted, (((0,), (0,)), ((), ())), preferred_element_type=jnp.float32
-    )
-    weight_part = weight_part.reshape((2,) * nbits + (in_chans // blocks, taps, out_chans))
     bits = [(axis, bit, combined) for combined, (axis, bit) in enumerate(index_bits(("rep", "tile")))]
-    bit_axes = list(range(nbits - 1, -1, -1))
+    streams = 3
+    per = taps // streams
+    parts = []
+    for s in range(streams):
+        cols = shifted[:, s * per * out_chans : (s + 1) * per * out_chans]
+        part = lax.dot_general(
+            flat_x, cols, (((0,), (0,)), ((), ())), preferred_element_type=jnp.float32
+        )
+        parts.append(part.reshape((2,) * nbits + (rows, per * out_chans)))
 
     accum_grad = lax.dot_general(
-        shifted,
+        shifted.reshape(local_pix, taps, out_chans),
         conv_weight,
         (((1, 2), (0, 2)), ((), ())),
         preferred_element_type=jnp.float32,
     )
     axis, bit, combined = bits[0]
+    bit_axes = list(range(nbits - 1, -1, -1))
     ax = bit_axes.index(combined)
     mine = (lax.axis_index(axis) >> bit) & 1
-    keep = lax.dynamic_index_in_dim(weight_part, mine, ax, keepdims=False)
-    send = lax.dynamic_index_in_dim(weight_part, 1 - mine, ax, keepdims=False)
-    received, accum_grad = lax.optimization_barrier((exchange(send, axis, bit), accum_grad))
-    half = keep + received
+    keeps = [lax.dynamic_index_in_dim(p, mine, ax, keepdims=False) for p in parts]
+    sends = [lax.dynamic_index_in_dim(p, 1 - mine, ax, keepdims=False) for p in parts]
+    received, accum_grad = lax.optimization_barrier(
+        ([exchange(v, axis, bit) for v in sends], accum_grad)
+    )
     bit_axes.pop(ax)
     rest = bits[1:]
-    streams = 3
-    per = taps // streams
     pieces = []
     for s in range(streams):
         order = rest[s:] + rest[:s]
-        chunk = lax.slice_in_dim(half, s * per, (s + 1) * per if s < streams - 1 else taps, axis=half.ndim - 2)
-        pieces.append(halving_scatter(chunk, order, bit_axes))
-    grad_weight = jnp.concatenate(pieces, 1)
+        pieces.append(halving_scatter(keeps[s] + received[s], order, bit_axes))
+    grad_weight = jnp.concatenate(pieces, 1).reshape(rows, taps, out_chans)
 
     grad_features = accum_grad.astype(jnp.bfloat16).reshape(images, tile_rows, columns, in_chans)
     return (grad_features, grad_weight, grad_gain, grad_shift, grad_class, loss)

time: 286 us -> 275 us (0.962)
  starting transfers between devices: 59.4 us -> 46.9 us
  waiting for transfers between devices: 72 us -> 81.7 us
  matrix products: 40.2 us -> 48.4 us
  local copies, waits for them, and re-layouts: 52.3 us -> 44.5 us
  blocking collectives: 26.9 us -> 20.8 us
    dynamic_slice x2, local copies, waits for them, and re-layouts: 19.7 us -> 1.27 us  [the longest x1 1.11 us: halving_scatter(): send = lax.dynamic_index_in_dim(x, 1 - mine, ax, keepdims=False)]
    ppermute x28 -> x30, starting transfers between devices: 54.9 us -> 44.1 us  [exchange(): return lax.ppermute(x, axis, pairs)]
    squeeze x0 -> x3, local copies, waits for them, and re-layouts: none -> 8.73 us  [body(): lax.dynamic_index_in_dim(p, 1 - mine, ax, keepdims=False)]
    ppermute x28 -> x30, waiting for transfers between devices: 70.2 us -> 78.5 us  [exchange(): return lax.ppermute(x, axis, pairs)]
    dot_general x2 -> x4, matrix products: 34.2 us -> 42.3 us  [the longest x3 23.6 us: body(): lax.dot_general(flat_x, cols, (((0,), (0,)), ((), ())), preferred_element...]
    psum x2 -> x1, blocking collectives: 14.7 us -> 8.37 us  [body(): lax.psum(jnp.concatenate([jnp.sum(yvals, 0), jnp.sum(weights_pix)[None]])...]
    slice x1, local copies, waits for them, and re-layouts: 5.27 us -> 0.52 us  [body(): column_sum, weight_tile = (first_sums[:out_chans], first_sums[out_chans])]
    dot_general x1 -> x3, local copies, waits for them, and re-layouts: 15.1 us -> 18.2 us  [body(): lax.dot_general(flat_x, cols, (((0,), (0,)), ((), ())), preferred_element...]
  transfers between devices with their start and end apart: 30 -> 32, of which waited for: 19 -> 18; matrix products, arithmetic and copies ran while one was open for 11% -> 28% of each run, Pallas kernels for 0% -> 0%
where the time goes in v3:
time: 275 us
  waiting for transfers between devices  81.7 us (30%)
  matrix products  48.4 us (18%)
  starting transfers between devices  46.9 us (17%)
  local copies, waits for them, and re-layouts  44.5 us (16%)
  other arithmetic  25 us (9%)
  blocking collectives  20.8 us (8%)
  between operations  7.43 us (3%)
    ppermute x30, waiting for transfers between devices, exchange(): return lax.ppermute(x, axis, pairs)  78.5 us
    ppermute x30, starting transfers between devices, exchange(): return lax.ppermute(x, axis, pairs)  44.1 us
    dot_general x3, matrix products, body(): lax.dot_general(flat_x, cols, (((0,), (0,)), ((), ())), preferred_element...  23.6 us
    dot_general x1, matrix products, body(): lax.dot_general(shifted.reshape(local_pix, taps, out_chans), conv_weight,...  18.7 us
    dot_general x3, local copies, waits for them, and re-layouts, body(): lax.dot_general(flat_x, cols, (((0,), (0,)), ((), ())), preferred_element...  18.2 us
    unnamed x65, local copies, waits for them, and re-layouts  9.77 us
    squeeze x3, local copies, waits for them, and re-layouts, body(): lax.dynamic_index_in_dim(p, 1 - mine, ax, keepdims=False)  8.73 us
    psum x1, blocking collectives, body(): lax.psum(jnp.concatenate([jnp.sum(yvals, 0), jnp.sum(weights_pix)[None]])...  8.37 us
  transfers between devices with their start and end apart: 32, of which 18 were waited for; matrix products, arithmetic and copies ran while one was open for 28% of the time, Pallas kernels for 0%

profile of v3, /device:TPU:0, one launch (start us, length us, event | category | flops | bytes accessed | tf_op | source)
XLA Modules:
  0.0 274.6 jit_solution(17231459136879847572)
XLA Ops:
  5.0 8.4 %psum.42 = f32[257]{0:T(512)S(1)} all-reduce(f32[257]{0:T(512)S(1)} %pad_maximum_fusion.1), channel_id=1, replica_groups=mesh['rep'=8,'tile'=4] {'tile'}, use_global_device_ids=true, to_apply=%region_2.0 | all-reduce | flops 257 | bytes 2056 | tf_op jit(solution)/shard_map/psum | solution.py:83
  16.8 5.8 %psum.43 = f32[256]{0:T(256)S(1)} all-reduce(f32[256]{0:T(256)S(1)} %multiply_reduce_fusion.1), channel_id=1, replica_groups=mesh['rep'=8,'tile'=4] {'tile'}, use_global_device_ids=true, to_apply=%region_4.0 | all-reduce | flops 256 | bytes 2048 | tf_op jit(solution)/shard_map/psum | solution.py:87
  31.0 4.0 %collective-permute-start.2 = (f32[]{:T(128)}, f32[]{:T(128)}, u32[]{:S(2)}, u32[]{:S(2)}) collective-permute-start(f32[]{:T(128)} %add.195), channel_id=1, source_target_pairs={{0,16},{4,20},{8,24},{12,28},{16,0},{20,4},{24,8},{28,12},{1,17},{... | collective-permute-start | bytes 20 | tf_op jit(solution)/shard_map/ppermute | solution.py:37
  37.8 3.3 %fusion.38 = (f32[256]{0:T(256)S(1)}, f32[256]{0:T(256)S(1)}, f32[1728,256]{1,0:T(8,128)}) fusion(f32[256]{0:T(256)S(1)} %get-tuple-element.50, f32[256]{0:T(256)S(1)} %slice_multiply_fusion, bf16[2,12,72,256]{3,2,1,0:T(8,128)(2,1)S(1)} %copy-done.2, f32[3,256]{1,0:T(4,128)S(1)} %copy-done, f32[1728,3]{0,1:T(4,128)S(1)} %get-tuple-element.52, ...), kind=kOutput, calls=%fused_computation.107 | convolution fusion | flops 20374336 | bytes 4474368 | tf_op jit(solution)/shard_map/dot_general | solution.py:100
  41.1 6.5 %all-reduce.1 = (f32[256]{0:T(256)S(1)}, f32[256]{0:T(256)S(1)}, f32[3,256]{1,0:T(4,128)}, f32[]{:T(128)}) all-reduce(f32[256]{0:T(256)S(1)} %get-tuple-element.27, f32[256]{0:T(256)S(1)} %get-tuple-element.26, f32[3,256]{1,0:T(4,128)S(1)} %fusion.22, f32[]{:T(128)} %get-tuple-element.36), channel_id=1, replica_groups=mesh['rep'=8,'tile'=4] {'tile'}, use_global_device_ids=true, to_apply=%region_11.12 | all-reduce | flops 1281 | bytes 10248 | tf_op jit(solution)/shard_map/psum | solution.py:102
  48.1 3.1 %collective-permute-done.23 = f32[256]{0:T(256)S(1)} collective-permute-done((f32[256]{0:T(256)S(1)}, f32[256]{0:T(256)S(1)}, u32[]{:S(2)}, u32[]{:S(2)}) %collective-permute-start.23) | collective-permute-done | bytes 1056 | tf_op jit(solution)/shard_map/ppermute | solution.py:37
  68.6 6.2 %convolution_bitcast_fusion.1 = f32[1536,768]{0,1:T(8,128)} fusion(bf16[1728,1536]{1,0:T(8,128)(2,1)S(1)} %bitcast.151, bf16[1728,256]{1,0:T(8,128)(2,1)S(1)} %bitcast.133, bf16[1728,256]{1,0:T(8,128)(2,1)S(1)} %bitcast.129, bf16[1728,256]{1,0:T(8,128)(2,1)S(1)} %bitcast.135), kind=kOutput, calls=%fused_computation.7 | convolution fusion | flops 4084826112 | bytes 12681216 | tf_op jit(solution)/shard_map/dot_general | solution.py:147
  74.8 6.1 %copy.22 = f32[1536,768]{1,0:T(8,128)} copy(f32[1536,768]{0,1:T(8,128)} %convolution_bitcast_fusion.1) | data formatting | bytes 9437184 | tf_op jit(solution)/shard_map/dot_general | solution.py:147
  80.9 3.4 %dynamic-slice_bitcast_fusion = f32[2,2,2,2,48,768]{5,4,3,2,1,0:T(8,128)} fusion(f32[2,2,2,2,2,48,768]{6,5,4,3,2,1,0:T(8,128)} %bitcast.114, s32[]{:T(128)S(6)} %select_n.65), kind=kLoop, calls=%fused_computation.31 | loop fusion | bytes 4718596 | tf_op jit(solution)/shard_map/jit(dynamic_index_in_dim)/squeeze | solution.py:163
  84.3 10.5 %collective-permute-start.7 = (f32[2,2,2,2,48,768]{5,4,3,2,1,0:T(8,128)}, f32[2,2,2,2,48,768]{5,4,3,2,1,0:T(8,128)}, u32[]{:S(2)}, u32[]{:S(2)}) collective-permute-start(f32[2,2,2,2,48,768]{5,4,3,2,1,0:T(8,128)} %dynamic-slice_bitcast_fusion), channel_id=1, source_target_pairs={{0,1},{1,0},{2,3},{3,2},{4,5},{5,4},{6,7},{7,6},{8,9},{9,8},{10,11... | collective-permute-start | bytes 7077896 | tf_op jit(solution)/shard_map/ppermute | solution.py:37
  94.8 8.7 %convolution_bitcast_fusion.2 = f32[1536,768]{0,1:T(8,128)} fusion(bf16[1728,1536]{1,0:T(8,128)(2,1)} %bitcast.147, bf16[1728,256]{1,0:T(8,128)(2,1)S(1)} %bitcast.137, bf16[1728,256]{1,0:T(8,128)(2,1)S(1)} %multiply_convert_fusion, bf16[1728,256]{1,0:T(8,128)(2,1)S(1)} %bitcast.144), kind=kOutput, calls=%fused_computation.8 | convolution fusion | flops 4084826112 | bytes 12681216 | tf_op jit(solution)/shard_map/dot_general | solution.py:147
  103.5 6.0 %copy.21 = f32[1536,768]{1,0:T(8,128)} copy(f32[1536,768]{0,1:T(8,128)} %convolution_bitcast_fusion.2) | data formatting | bytes 9437184 | tf_op jit(solution)/shard_map/dot_general | solution.py:147
  109.6 3.4 %dynamic-slice_bitcast_fusion.1 = f32[2,2,2,2,48,768]{5,4,3,2,1,0:T(8,128)} fusion(f32[2,2,2,2,2,48,768]{6,5,4,3,2,1,0:T(8,128)} %bitcast.118, s32[]{:T(128)S(6)} %select_n.65), kind=kLoop, calls=%fused_computation.32 | loop fusion | bytes 4718596 | tf_op jit(solution)/shard_map/jit(dynamic_index_in_dim)/squeeze | solution.py:163
  113.0 8.7 %convolution_bitcast_fusion.3 = f32[1536,768]{0,1:T(8,128)} fusion(bf16[1728,1536]{1,0:T(8,128)(2,1)} %bitcast.148, bf16[1728,256]{1,0:T(8,128)(2,1)S(1)} %bitcast.140, bf16[1728,256]{1,0:T(8,128)(2,1)S(1)} %bitcast.132, bf16[1728,256]{1,0:T(8,128)(2,1)S(1)} %bitcast.142), kind=kOutput, calls=%fused_computation.9 | convolution fusion | flops 4084826112 | bytes 12681216 | tf_op jit(solution)/shard_map/dot_general | solution.py:147
  121.7 6.1 %copy.20 = f32[1536,768]{1,0:T(8,128)} copy(f32[1536,768]{0,1:T(8,128)} %convolution_bitcast_fusion.3) | data formatting | bytes 9437184 | tf_op jit(solution)/shard_map/dot_general | solution.py:147
  134.3 18.7 %convolution_bitcast_fusion = bf16[1728,1536]{1,0:T(8,128)(2,1)} fusion(bf16[1728,9,256]{2,0,1:T(8,128)(2,1)} %constant_dynamic-update-slice_fusion, bf16[9,1536,256]{2,1,0:T(8,128)(2,1)} %param.10), kind=kOutput, calls=%fused_computation.2 | convolution fusion | flops 12230590464 | bytes 20348928 | tf_op jit(solution)/shard_map/dot_general | solution.py:152
  165.2 21.4 %collective-permute-done.26 = f32[3,256]{1,0:T(4,128)S(1)} collective-permute-done((f32[3,256]{1,0:T(4,128)S(1)}, f32[3,256]{1,0:T(4,128)S(1)}, u32[]{:S(2)}, u32[]{:S(2)}) %collective-permute-start.26) | collective-permute-done | bytes 3104 | tf_op jit(solution)/shard_map/ppermute | solution.py:37
  188.8 3.3 %collective-permute-done.29 = f32[]{:T(128)} collective-permute-done((f32[]{:T(128)}, f32[]{:T(128)}, u32[]{:S(2)}, u32[]{:S(2)}) %collective-permute-start.29) | collective-permute-done | bytes 36 | tf_op jit(solution)/shard_map/ppermute | solution.py:37
  200.5 3.9 %collective-permute-start.31 = (f32[]{:T(128)}, f32[]{:T(128)}, u32[]{:S(2)}, u32[]{:S(2)}) collective-permute-start(f32[]{:T(128)} %add.233), channel_id=1, source_target_pairs={{0,16},{4,20},{8,24},{12,28},{16,0},{20,4},{24,8},{28,12},{1,17},{... | collective-permute-start | bytes 20 | tf_op jit(solution)/shard_map/ppermute | solution.py:37
  212.2 3.3 %collective-permute-done.22 = f32[256]{0:T(256)S(1)} collective-permute-done((f32[256]{0:T(256)S(1)}, f32[256]{0:T(256)S(1)}, u32[]{:S(2)}, u32[]{:S(2)}) %collective-permute-start.22) | collective-permute-done | bytes 1056 | tf_op jit(solution)/shard_map/ppermute | solution.py:37
  229.9 4.2 %collective-permute-done.9 = f32[2,2,48,768]{3,2,1,0:T(8,128)S(1)} collective-permute-done((f32[2,2,48,768]{3,2,1,0:T(8,128)S(1)}, f32[2,2,48,768]{3,2,1,0:T(8,128)S(1)}, u32[]{:S(2)}, u32[]{:S(2)}) %collective-permute-start.9) | collective-permute-done | bytes 589856 | tf_op jit(solution)/shard_map/ppermute | solution.py:37
  234.8 14.6 %collective-permute-done.13 = f32[2,2,48,768]{3,2,1,0:T(8,128)S(1)} collective-permute-done((f32[2,2,48,768]{3,2,1,0:T(8,128)S(1)}, f32[2,2,48,768]{3,2,1,0:T(8,128)S(1)}, u32[]{:S(2)}, u32[]{:S(2)}) %collective-permute-start.13) | collective-permute-done | bytes 589856 | tf_op jit(solution)/shard_map/ppermute | solution.py:37
  249.6 10.9 %collective-permute-done.17 = f32[2,2,48,768]{3,2,1,0:T(8,128)S(1)} collective-permute-done((f32[2,2,48,768]{3,2,1,0:T(8,128)S(1)}, f32[2,2,48,768]{3,2,1,0:T(8,128)S(1)}, u32[]{:S(2)}, u32[]{:S(2)}) %collective-permute-start.17) | collective-permute-done | bytes 589856 | tf_op jit(solution)/shard_map/ppermute | solution.py:37
  269.0 3.6 %collective-permute-done.19 = f32[48,768]{1,0:T(8,128)S(1)} collective-permute-done((f32[48,768]{1,0:T(8,128)S(1)}, f32[48,768]{1,0:T(8,128)S(1)}, u32[]{:S(2)}, u32[]{:S(2)}) %collective-permute-start.19) | collective-permute-done | bytes 147488 | tf_op jit(solution)/shard_map/ppermute | solution.py:37
  (180 shorter events, 93.0 us)
Async XLA Ops:
  13.9 11.5 %collective-permute-start = (f32[]{:T(128)}, f32[]{:T(128)}, u32[]{:S(2)}, u32[]{:S(2)}) collective-permute-start(f32[]{:T(128)} %bitcast.2), channel_id=1, source_target_pairs={{0,4},{4,0},{8,12},{12,8},{16,20},{20,16},{24,28},{28,24},{1,5},{5... | collective-permute-start | bytes 20 | tf_op jit(solution)/shard_map/ppermute | solution.py:37
  31.0 4.6 %collective-permute-start.2 = (f32[]{:T(128)}, f32[]{:T(128)}, u32[]{:S(2)}, u32[]{:S(2)}) collective-permute-start(f32[]{:T(128)} %add.195), channel_id=1, source_target_pairs={{0,16},{4,20},{8,24},{12,28},{16,0},{20,4},{24,8},{28,12},{1,17},{... | collective-permute-start | bytes 20 | tf_op jit(solution)/shard_map/ppermute | solution.py:37
  55.2 4.7 %collective-permute-start.4 = (bf16[2,12,72,256]{3,2,1,0:T(8,128)(2,1)S(1)}, bf16[2,12,72,256]{3,2,1,0:T(8,128)(2,1)S(1)}, u32[]{:S(2)}, u32[]{:S(2)}) collective-permute-start(bf16[2,12,72,256]{3,2,1,0:T(8,128)(2,1)S(1)} %bitcast.127), channel_id=1, source_target_pairs={{1,0},{2,1},{3,2},{5,4},{6,5},{7,6},{9,8},{10,9},{11,10},{13,12},{... | collective-permute-start | bytes 2654216 | tf_op jit(solution)/shard_map/ppermute | solution.py:20
  84.3 68.7 %collective-permute-start.7 = (f32[2,2,2,2,48,768]{5,4,3,2,1,0:T(8,128)}, f32[2,2,2,2,48,768]{5,4,3,2,1,0:T(8,128)}, u32[]{:S(2)}, u32[]{:S(2)}) collective-permute-start(f32[2,2,2,2,48,768]{5,4,3,2,1,0:T(8,128)} %dynamic-slice_bitcast_fusion), channel_id=1, source_target_pairs={{0,1},{1,0},{2,3},{3,2},{4,5},{5,4},{6,7},{7,6},{8,9},{9,8},{10,11... | collective-permute-start | bytes 7077896 | tf_op jit(solution)/shard_map/ppermute | solution.py:37
  113.0 40.1 %collective-permute-start.6 = (f32[2,2,2,2,48,768]{5,4,3,2,1,0:T(8,128)}, f32[2,2,2,2,48,768]{5,4,3,2,1,0:T(8,128)}, u32[]{:S(2)}, u32[]{:S(2)}) collective-permute-start(f32[2,2,2,2,48,768]{5,4,3,2,1,0:T(8,128)} %dynamic-slice_bitcast_fusion.1), channel_id=1, source_target_pairs={{0,1},{1,0},{2,3},{3,2},{4,5},{5,4},{6,7},{7,6},{8,9},{9,8},{10,11... | collective-permute-start | bytes 7077896 | tf_op jit(solution)/shard_map/ppermute | solution.py:37
  129.7 23.3 %collective-permute-start.5 = (f32[2,2,2,2,48,768]{5,4,3,2,1,0:T(8,128)S(1)}, f32[2,2,2,2,48,768]{5,4,3,2,1,0:T(8,128)S(1)}, u32[]{:S(2)}, u32[]{:S(2)}) collective-permute-start(f32[2,2,2,2,48,768]{5,4,3,2,1,0:T(8,128)S(1)} %dynamic-slice_bitcast_fusion.2), channel_id=1, source_target_pairs={{0,1},{1,0},{2,3},{3,2},{4,5},{5,4},{6,7},{7,6},{8,9},{9,8},{10,11... | collective-permute-start | bytes 7077896 | tf_op jit(solution)/shard_map/ppermute | solution.py:37
  154.7 67.8 %collective-permute-start.8 = (f32[2,2,2,48,768]{4,3,1,0,2:T(8,128)}, f32[2,2,2,48,768]{4,3,1,0,2:T(8,128)}, u32[]{:S(2)}, u32[]{:S(2)}) collective-permute-start(f32[2,2,2,48,768]{4,3,1,0,2:T(8,128)} %bitcast.112), channel_id=1, source_target_pairs={{0,2},{1,3},{2,0},{3,1},{4,6},{5,7},{6,4},{7,5},{8,10},{9,11},{10,... | collective-permute-start | bytes 3538952 | tf_op jit(solution)/shard_map/ppermute | solution.py:37
  158.5 66.3 %collective-permute-start.12 = (f32[2,2,2,48,768]{4,3,2,1,0:T(8,128)}, f32[2,2,2,48,768]{4,3,2,1,0:T(8,128)}, u32[]{:S(2)}, u32[]{:S(2)}) collective-permute-start(f32[2,2,2,48,768]{4,3,2,1,0:T(8,128)} %dynamic-slice_bitcast_fusion.4), channel_id=1, source_target_pairs={{0,4},{4,0},{8,12},{12,8},{16,20},{20,16},{24,28},{28,24},{1,5},{5... | collective-permute-start | bytes 3538952 | tf_op jit(solution)/shard_map/ppermute | solution.py:37
  162.0 64.7 %collective-permute-start.16 = (f32[2,2,2,48,768]{4,3,2,1,0:T(8,128)}, f32[2,2,2,48,768]{4,3,2,1,0:T(8,128)}, u32[]{:S(2)}, u32[]{:S(2)}) collective-permute-start(f32[2,2,2,48,768]{4,3,2,1,0:T(8,128)} %dynamic-slice_bitcast_fusion.3), channel_id=1, source_target_pairs={{0,8},{4,12},{8,0},{12,4},{16,24},{20,28},{24,16},{28,20},{1,9},{5... | collective-permute-start | bytes 3538952 | tf_op jit(solution)/shard_map/ppermute | solution.py:37
  163.7 22.9 %collective-permute-start.26 = (f32[3,256]{1,0:T(4,128)S(1)}, f32[3,256]{1,0:T(4,128)S(1)}, u32[]{:S(2)}, u32[]{:S(2)}) collective-permute-start(f32[3,256]{1,0:T(4,128)S(1)} %copy-done.17), channel_id=1, source_target_pairs={{0,4},{4,0},{8,12},{12,8},{16,20},{20,16},{24,28},{28,24},{1,5},{5... | collective-permute-start | bytes 9224 | tf_op jit(solution)/shard_map/ppermute | solution.py:37
  186.7 18.8 %collective-permute-start.27 = (f32[3,256]{1,0:T(4,128)S(1)}, f32[3,256]{1,0:T(4,128)S(1)}, u32[]{:S(2)}, u32[]{:S(2)}) collective-permute-start(f32[3,256]{1,0:T(4,128)S(1)} %add.229), channel_id=1, source_target_pairs={{0,8},{4,12},{8,0},{12,4},{16,24},{20,28},{24,16},{28,20},{1,9},{5... | collective-permute-start | bytes 9224 | tf_op jit(solution)/shard_map/ppermute | solution.py:37
  200.5 4.6 %collective-permute-start.31 = (f32[]{:T(128)}, f32[]{:T(128)}, u32[]{:S(2)}, u32[]{:S(2)}) collective-permute-start(f32[]{:T(128)} %add.233), channel_id=1, source_target_pairs={{0,16},{4,20},{8,24},{12,28},{16,0},{20,4},{24,8},{28,12},{1,17},{... | collective-permute-start | bytes 20 | tf_op jit(solution)/shard_map/ppermute | solution.py:37
  205.5 5.5 %collective-permute-start.24 = (f32[256]{0:T(256)S(1)}, f32[256]{0:T(256)S(1)}, u32[]{:S(2)}, u32[]{:S(2)}) collective-permute-start(f32[256]{0:T(256)S(1)} %copy-done.18), channel_id=1, source_target_pairs={{0,8},{4,12},{8,0},{12,4},{16,24},{20,28},{24,16},{28,20},{1,9},{5... | collective-permute-start | bytes 3080 | tf_op jit(solution)/shard_map/ppermute | solution.py:37
  208.6 13.3 %collective-permute-start.28 = (f32[3,256]{1,0:T(4,128)S(1)}, f32[3,256]{1,0:T(4,128)S(1)}, u32[]{:S(2)}, u32[]{:S(2)}) collective-permute-start(f32[3,256]{1,0:T(4,128)S(1)} %add.230), channel_id=1, source_target_pairs={{0,16},{4,20},{8,24},{12,28},{16,0},{20,4},{24,8},{28,12},{1,17},{... | collective-permute-start | bytes 9224 | tf_op jit(solution)/shard_map/ppermute | solution.py:37
  216.1 4.6 %collective-permute-start.25 = (f32[256]{0:T(256)S(1)}, f32[256]{0:T(256)}, u32[]{:S(2)}, u32[]{:S(2)}) collective-permute-start(f32[256]{0:T(256)S(1)} %add.227), channel_id=1, source_target_pairs={{0,16},{4,20},{8,24},{12,28},{16,0},{20,4},{24,8},{28,12},{1,17},{... | collective-permute-start | bytes 3080 | tf_op jit(solution)/shard_map/ppermute | solution.py:37
  224.2 9.9 %collective-permute-start.9 = (f32[2,2,48,768]{3,2,1,0:T(8,128)S(1)}, f32[2,2,48,768]{3,2,1,0:T(8,128)S(1)}, u32[]{:S(2)}, u32[]{:S(2)}) collective-permute-start(f32[2,2,48,768]{3,2,1,0:T(8,128)S(1)} %dynamic-slice_bitcast_fusion.7), channel_id=1, source_target_pairs={{0,4},{4,0},{8,12},{12,8},{16,20},{20,16},{24,28},{28,24},{1,5},{5... | collective-permute-start | bytes 1769480 | tf_op jit(solution)/shard_map/ppermute | solution.py:37
  226.2 23.1 %collective-permute-start.13 = (f32[2,2,48,768]{3,2,1,0:T(8,128)S(1)}, f32[2,2,48,768]{3,2,1,0:T(8,128)S(1)}, u32[]{:S(2)}, u32[]{:S(2)}) collective-permute-start(f32[2,2,48,768]{3,2,1,0:T(8,128)S(1)} %dynamic-slice_bitcast_fusion.6), channel_id=1, source_target_pairs={{0,8},{4,12},{8,0},{12,4},{16,24},{20,28},{24,16},{28,20},{1,9},{5... | collective-permute-start | bytes 1769480 | tf_op jit(solution)/shard_map/ppermute | solution.py:37
  228.3 32.1 %collective-permute-start.17 = (f32[2,2,48,768]{3,2,1,0:T(8,128)S(1)}, f32[2,2,48,768]{3,2,1,0:T(8,128)S(1)}, u32[]{:S(2)}, u32[]{:S(2)}) collective-permute-start(f32[2,2,48,768]{3,2,1,0:T(8,128)S(1)} %dynamic-slice_bitcast_fusion.5), channel_id=1, source_target_pairs={{0,16},{4,20},{8,24},{12,28},{16,0},{20,4},{24,8},{28,12},{1,17},{... | collective-permute-start | bytes 1769480 | tf_op jit(solution)/shard_map/ppermute | solution.py:37
  234.3 27.2 %collective-permute-start.10 = (f32[2,48,768]{2,1,0:T(8,128)S(1)}, f32[2,48,768]{2,1,0:T(8,128)S(1)}, u32[]{:S(2)}, u32[]{:S(2)}) collective-permute-start(f32[2,48,768]{2,1,0:T(8,128)S(1)} %dynamic-slice_bitcast_fusion.10), channel_id=1, source_target_pairs={{0,8},{4,12},{8,0},{12,4},{16,24},{20,28},{24,16},{28,20},{1,9},{5... | collective-permute-start | bytes 884744 | tf_op jit(solution)/shard_map/ppermute | solution.py:37
  249.5 14.1 %collective-permute-start.14 = (f32[2,48,768]{2,1,0:T(8,128)S(1)}, f32[2,48,768]{2,1,0:T(8,128)S(1)}, u32[]{:S(2)}, u32[]{:S(2)}) collective-permute-start(f32[2,48,768]{2,1,0:T(8,128)S(1)} %dynamic-slice_bitcast_fusion.9), channel_id=1, source_target_pairs={{0,16},{4,20},{8,24},{12,28},{16,0},{20,4},{24,8},{28,12},{1,17},{... | collective-permute-start | bytes 884744 | tf_op jit(solution)/shard_map/ppermute | solution.py:37
  260.6 6.8 %collective-permute-start.18 = (f32[2,48,768]{2,1,0:T(8,128)S(1)}, f32[2,48,768]{2,1,0:T(8,128)S(1)}, u32[]{:S(2)}, u32[]{:S(2)}) collective-permute-start(f32[2,48,768]{2,1,0:T(8,128)S(1)} %dynamic-slice_bitcast_fusion.8), channel_id=1, source_target_pairs={{0,2},{1,3},{2,0},{3,1},{4,6},{5,7},{6,4},{7,5},{8,10},{9,11},{10,... | collective-permute-start | bytes 884744 | tf_op jit(solution)/shard_map/ppermute | solution.py:37
  261.5 7.5 %collective-permute-start.11 = (f32[48,768]{1,0:T(8,128)S(1)}, f32[48,768]{1,0:T(8,128)S(1)}, u32[]{:S(2)}, u32[]{:S(2)}) collective-permute-start(f32[48,768]{1,0:T(8,128)S(1)} %dynamic-slice_bitcast_fusion.13), channel_id=1, source_target_pairs={{0,16},{4,20},{8,24},{12,28},{16,0},{20,4},{24,8},{28,12},{1,17},{... | collective-permute-start | bytes 442376 | tf_op jit(solution)/shard_map/ppermute | solution.py:37
  263.7 5.3 %collective-permute-start.15 = (f32[48,768]{1,0:T(8,128)S(1)}, f32[48,768]{1,0:T(8,128)S(1)}, u32[]{:S(2)}, u32[]{:S(2)}) collective-permute-start(f32[48,768]{1,0:T(8,128)S(1)} %dynamic-slice_bitcast_fusion.12), channel_id=1, source_target_pairs={{0,2},{1,3},{2,0},{3,1},{4,6},{5,7},{6,4},{7,5},{8,10},{9,11},{10,... | collective-permute-start | bytes 442376 | tf_op jit(solution)/shard_map/ppermute | solution.py:37
  267.4 5.2 %collective-permute-start.19 = (f32[48,768]{1,0:T(8,128)S(1)}, f32[48,768]{1,0:T(8,128)S(1)}, u32[]{:S(2)}, u32[]{:S(2)}) collective-permute-start(f32[48,768]{1,0:T(8,128)S(1)} %dynamic-slice_bitcast_fusion.11), channel_id=1, source_target_pairs={{0,4},{4,0},{8,12},{12,8},{16,20},{20,16},{24,28},{28,24},{1,5},{5... | collective-permute-start | bytes 442376 | tf_op jit(solution)/shard_map/ppermute | solution.py:37
  (36 other events, 346.6 us)

commit v4 on v3

--- a/solution.py
+++ b/solution.py
@@ -108,10 +108,10 @@
         ),
         "tile",
     )
-    grad_shift, grad_gain, grad_class, loss_total = butterfly_sum(
-        (first_gradient_sum, second_gradient_sum, class_tile, loss_tile), ("rep",)
+    packed = jnp.concatenate(
+        [first_gradient_sum, second_gradient_sum, class_tile.reshape(-1), loss_tile[None]]
     )
-    loss = loss_total / mean_weight / all_pix
+    packed = butterfly_sum(packed, ("rep",))
     normalized_output_gradient = (
         norm_gain_vector
         * inverse_deviation
@@ -133,21 +133,28 @@
         piece = extended[:, row_off : row_off + tile_rows, col_off : col_off + columns, :]
         shifted_list.append(piece.reshape(local_pix, out_chans))
     shifted = jnp.concatenate(shifted_list, 1)
+    packed, shifted = lax.optimization_barrier((packed, shifted))
+    grad_shift = packed[:out_chans]
+    grad_gain = packed[out_chans : 2 * out_chans]
+    grad_class = packed[2 * out_chans : (2 + classes) * out_chans].reshape(classes, out_chans)
+    loss = packed[(2 + classes) * out_chans] / mean_weight / all_pix
 
     blocks = lax.axis_size("rep") * lax.axis_size("tile")
     nbits = blocks.bit_length() - 1
     rows = in_chans // blocks
     flat_x = features.reshape(local_pix, in_chans)
     bits = [(axis, bit, combined) for combined, (axis, bit) in enumerate(index_bits(("rep", "tile")))]
-    streams = 3
-    per = taps // streams
+    rest = bits[1:]
+    orders = [rest, rest[1:2] + rest[:1] + rest[2:], rest[2:] + rest[:2]]
+    group_taps = [taps - 2 * (taps // 3) + 1, taps // 3, taps // 3 - 1]
+    starts = [sum(group_taps[:s]) for s in range(3)]
     parts = []
-    for s in range(streams):
-        cols = shifted[:, s * per * out_chans : (s + 1) * per * out_chans]
+    for s in range(3):
+        cols = shifted[:, starts[s] * out_chans : (starts[s] + group_taps[s]) * out_chans]
         part = lax.dot_general(
             flat_x, cols, (((0,), (0,)), ((), ())), preferred_element_type=jnp.float32
         )
-        parts.append(part.reshape((2,) * nbits + (rows, per * out_chans)))
+        parts.append(part.reshape((2,) * nbits + (rows, group_taps[s] * out_chans)))
 
     accum_grad = lax.dot_general(
         shifted.reshape(local_pix, taps, out_chans),
@@ -165,11 +172,9 @@
         ([exchange(v, axis, bit) for v in sends], accum_grad)
     )
     bit_axes.pop(ax)
-    rest = bits[1:]
     pieces = []
-    for s in range(streams):
-        order = rest[s:] + rest[:s]
-        pieces.append(halving_scatter(keeps[s] + received[s], order, bit_axes))
+    for s in range(3):
+        pieces.append(halving_scatter(keeps[s] + received[s], orders[s], bit_axes))
     grad_weight = jnp.concatenate(pieces, 1).reshape(rows, taps, out_chans)
 
     grad_features = accum_grad.astype(jnp.bfloat16).reshape(images, tile_rows, columns, in_chans)

time: 275 us -> 245 us (0.89)
  waiting for transfers between devices: 81.7 us -> 62.9 us
  starting transfers between devices: 46.9 us -> 37.1 us
  local copies, waits for them, and re-layouts: 44.5 us -> 50.4 us
  matrix products: 48.4 us -> 44.4 us
    ppermute x30 -> x21, waiting for transfers between devices: 78.5 us -> 62.9 us  [exchange(): return lax.ppermute(x, axis, pairs)]
    optimization_barrier x0 -> x1, local copies, waits for them, and re-layouts: none -> 11.6 us  [body(): packed, shifted = lax.optimization_barrier((packed, shifted))]
    ppermute x30 -> x21, starting transfers between devices: 44.1 us -> 32.6 us  [exchange(): return lax.ppermute(x, axis, pairs)]
    add x9 -> x3, other arithmetic: 5 us -> 0.01 us  [butterfly_sum(): x = jax.tree.map(lambda v, w: v + w, x, exchange(x, axis, bit))]
    dot_general x3, matrix products: 23.6 us -> 18.8 us  [body(): lax.dot_general(flat_x, cols, (((0,), (0,)), ((), ())), preferred_element...]
    unnamed x65 -> x41, local copies, waits for them, and re-layouts: 9.77 us -> 6.44 us
    dot_general x3, local copies, waits for them, and re-layouts: 18.2 us -> 15.1 us  [body(): lax.dot_general(flat_x, cols, (((0,), (0,)), ((), ())), preferred_element...]
    add x12, other arithmetic: 4.91 us -> 8.04 us  [halving_scatter(): x = keep + exchange(send, axis, bit)]
  transfers between devices with their start and end apart: 32 -> 23, of which waited for: 18 -> 11; matrix products, arithmetic and copies ran while one was open for 28% -> 26% of each run, Pallas kernels for 0% -> 0%
where the time goes in v4:
time: 245 us; the launch traced here: 244 us
  waiting for transfers between devices  62.9 us (26%)
  local copies, waits for them, and re-layouts  50.4 us (21%)
  matrix products  44.4 us (18%)
  starting transfers between devices  37.1 us (15%)
  other arithmetic  23.5 us (10%)
  blocking collectives  20.7 us (8%)
  between operations  5.24 us (2%)
    ppermute x21, waiting for transfers between devices, exchange(): return lax.ppermute(x, axis, pairs)  62.9 us
    ppermute x21, starting transfers between devices, exchange(): return lax.ppermute(x, axis, pairs)  32.6 us
    dot_general x1, matrix products, body(): lax.dot_general(shifted.reshape(local_pix, taps, out_chans), conv_weight,...  19.5 us
    dot_general x3, matrix products, body(): lax.dot_general(flat_x, cols, (((0,), (0,)), ((), ())), preferred_element...  18.8 us
    dot_general x3, local copies, waits for them, and re-layouts, body(): lax.dot_general(flat_x, cols, (((0,), (0,)), ((), ())), preferred_element...  15.1 us
    optimization_barrier x1, local copies, waits for them, and re-layouts, body(): packed, shifted = lax.optimization_barrier((packed, shifted))  11.6 us
    psum x1, blocking collectives, body(): lax.psum(jnp.concatenate([jnp.sum(yvals, 0), jnp.sum(weights_pix)[None]])...  8.37 us
    add x12, other arithmetic, halving_scatter(): x = keep + exchange(send, axis, bit)  8.04 us
  transfers between devices with their start and end apart: 23, of which 11 were waited for; matrix products, arithmetic and copies ran while one was open for 26% of the time, Pallas kernels for 0%

profile of v4, /device:TPU:0, one launch (start us, length us, event | category | flops | bytes accessed | tf_op | source)
XLA Modules:
  0.0 244.2 jit_solution(10572240548500424688)
XLA Ops:
  5.0 8.4 %psum.42 = f32[257]{0:T(512)S(1)} all-reduce(f32[257]{0:T(512)S(1)} %pad_maximum_fusion.1), channel_id=1, replica_groups=mesh['rep'=8,'tile'=4] {'tile'}, use_global_device_ids=true, to_apply=%region_2.0 | all-reduce | flops 257 | bytes 2056 | tf_op jit(solution)/shard_map/psum | solution.py:83
  16.8 5.8 %psum.43 = f32[256]{0:T(256)S(1)} all-reduce(f32[256]{0:T(256)S(1)} %multiply_reduce_fusion.1), channel_id=1, replica_groups=mesh['rep'=8,'tile'=4] {'tile'}, use_global_device_ids=true, to_apply=%region_4.0 | all-reduce | flops 256 | bytes 2048 | tf_op jit(solution)/shard_map/psum | solution.py:87
  30.8 4.0 %collective-permute-start.2 = (f32[]{:T(128)}, f32[]{:T(128)}, u32[]{:S(2)}, u32[]{:S(2)}) collective-permute-start(f32[]{:T(128)} %add.173), channel_id=1, source_target_pairs={{0,16},{4,20},{8,24},{12,28},{16,0},{20,4},{24,8},{28,12},{1,17},{... | collective-permute-start | bytes 20 | tf_op jit(solution)/shard_map/ppermute | solution.py:37
  37.6 3.3 %multiply_reduce_fusion = (f32[256]{0:T(256)S(1)}, f32[256]{0:T(256)S(1)}, f32[1728,256]{1,0:T(8,128)}) fusion(f32[256]{0:T(256)S(1)} %get-tuple-element.56, f32[256]{0:T(256)S(1)} %slice_multiply_fusion, bf16[2,12,72,256]{3,2,1,0:T(8,128)(2,1)S(1)} %copy-done.2, f32[3,256]{1,0:T(4,128)S(1)} %copy-done, f32[1728,3]{0,1:T(4,128)S(1)} %get-tuple-element.60, ...), kind=kOutput, calls=%fused_computation.23 | convolution fusion | flops 20374336 | bytes 4474368 | tf_op jit(solution)/shard_map/dot_general | solution.py:100
  40.9 6.5 %all-reduce.1 = (f32[256]{0:T(256)S(1)}, f32[256]{0:T(256)S(1)}, f32[768]{0:T(1024)S(1)}, f32[1]{0:T(128)}) all-reduce(f32[256]{0:T(256)S(1)} %get-tuple-element.31, f32[256]{0:T(256)S(1)} %get-tuple-element.30, f32[768]{0:T(1024)S(1)} %reshape.96, f32[1]{0:T(128)} %bitcast.3), channel_id=1, replica_groups=mesh['rep'=8,'tile'=4] {'tile'}, use_global_device_ids=true, to_apply=%region_9.10 | all-reduce | flops 1281 | bytes 10248 | tf_op jit(solution)/shard_map/psum | solution.py:102
  50.7 3.3 %collective-permute-start.6 = (bf16[2,12,72,256]{3,2,1,0:T(8,128)(2,1)S(1)}, bf16[2,12,72,256]{3,2,1,0:T(8,128)(2,1)S(1)}, u32[]{:S(2)}, u32[]{:S(2)}) collective-permute-start(bf16[2,12,72,256]{3,2,1,0:T(8,128)(2,1)S(1)} %bitcast.120), channel_id=1, source_target_pairs={{0,1},{1,2},{2,3},{4,5},{5,6},{6,7},{8,9},{9,10},{10,11},{12,13},{... | collective-permute-start | bytes 2654216 | tf_op jit(solution)/shard_map/ppermute | solution.py:19
  55.2 3.2 %collective-permute-done.3 = f32[1281]{0:T(1024)S(1)} collective-permute-done((f32[1281]{0:T(1024)S(1)}, f32[1281]{0:T(1024)S(1)}, u32[]{:S(2)}, u32[]{:S(2)}) %collective-permute-start.3) | collective-permute-done | bytes 5156 | tf_op jit(solution)/shard_map/ppermute | solution.py:37
  70.4 3.7 %slice-done.5 = s8[4194304]{0:T(1024)(128)(4,1)S(1)} async-done(((s8[5308416]{0:T(1024)(128)(4,1)}), s8[4194304]{0:T(1024)(128)(4,1)S(1)}, s32[]{:S(2)}) %slice-start.5) | async-done | bytes 4194328
  74.1 4.8 %convolution_bitcast_fusion.3 = f32[1536,512]{0,1:T(8,128)} fusion(bf16[1728,1536]{1,0:T(8,128)(2,1)S(1)} %bitcast.134, bf16[1728,2304]{1,0:T(8,128)(2,1)S(1)} %constant_dynamic-update-slice_fusion.1), kind=kOutput, calls=%fused_computation.12 | convolution fusion | flops 2717908992 | bytes 10223616 | tf_op jit(solution)/shard_map/dot_general | solution.py:154
  78.9 6.1 %convolution_bitcast_fusion.2 = f32[1536,768]{0,1:T(8,128)} fusion(bf16[1728,1536]{1,0:T(8,128)(2,1)S(1)} %bitcast.135, bf16[1728,2304]{1,0:T(8,128)(2,1)S(1)} %constant_dynamic-update-slice_fusion.1), kind=kOutput, calls=%fused_computation.8 | convolution fusion | flops 4076863488 | bytes 12681216 | tf_op jit(solution)/shard_map/dot_general | solution.py:154
  85.0 7.9 %convolution_bitcast_fusion.1 = f32[1536,1024]{0,1:T(8,128)} fusion(bf16[1728,1536]{1,0:T(8,128)(2,1)S(1)} %bitcast.136, bf16[1728,2304]{1,0:T(8,128)(2,1)S(1)} %constant_dynamic-update-slice_fusion.1), kind=kOutput, calls=%fused_computation.4 | convolution fusion | flops 5435817984 | bytes 15138816 | tf_op jit(solution)/shard_map/dot_general | solution.py:154
  95.3 6.6 %copy.23 = f32[1536,1024]{1,0:T(8,128)} copy(f32[1536,1024]{0,1:T(8,128)} %convolution_bitcast_fusion.1) | data formatting | bytes 12582912 | tf_op jit(solution)/shard_map/dot_general | solution.py:154
  101.9 3.9 %dynamic-slice_bitcast_fusion = f32[2,2,2,2,48,1024]{5,4,3,2,1,0:T(8,128)} fusion(f32[2,2,2,2,2,48,1024]{6,5,4,3,2,1,0:T(8,128)} %bitcast.108, s32[]{:T(128)S(6)} %select_n.70), kind=kLoop, calls=%fused_computation.14 | loop fusion | bytes 6291460 | tf_op jit(solution)/shard_map/jit(dynamic_index_in_dim)/squeeze | solution.py:170
  107.2 11.6 %copy.26 = bf16[1728,2304]{0,1:T(8,128)(2,1)} copy(bf16[1728,2304]{1,0:T(8,128)(2,1)} %copy-done.3) | data formatting | bytes 15925248 | tf_op jit(solution)/shard_map/optimization_barrier | solution.py:136
  119.3 6.1 %copy.24 = f32[1536,768]{1,0:T(8,128)} copy(f32[1536,768]{0,1:T(8,128)} %convolution_bitcast_fusion.2) | data formatting | bytes 9437184 | tf_op jit(solution)/shard_map/dot_general | solution.py:154
  127.3 19.5 %convolution_bitcast_fusion = bf16[1728,1536]{1,0:T(8,128)(2,1)} fusion(bf16[1728,9,256]{0,2,1:T(8,128)(2,1)} %bitcast.118, bf16[9,1536,256]{2,1,0:T(8,128)(2,1)} %param.10), kind=kOutput, calls=%fused_computation.2 | convolution fusion | flops 12230590464 | bytes 20348928 | tf_op jit(solution)/shard_map/dot_general | solution.py:159
  152.5 2.9 %bitcast_add_fusion = f32[2,2,2,2,48,1024]{5,4,3,2,1,0:T(8,128)S(1)} fusion(f32[2,2,2,2,48,1024]{5,4,3,2,1,0:T(8,128)} %collective-permute-done.8, f32[2,2,2,2,2,48,1024]{6,5,4,3,2,1,0:T(8,128)S(1)} %bitcast.111, s32[]{:T(128)S(6)} %select_n.71), kind=kLoop, calls=%fused_computation.13 | loop fusion | flops 786432 | bytes 9437188 | tf_op jit(solution)/shard_map/add | solution.py:177
  157.9 10.6 %collective-permute-done.19 = f32[2,2,2,48,512]{4,3,2,1,0:T(8,128)S(1)} collective-permute-done((f32[2,2,2,48,512]{4,3,2,1,0:T(8,128)S(1)}, f32[2,2,2,48,512]{4,3,2,1,0:T(8,128)S(1)}, u32[]{:S(2)}, u32[]{:S(2)}) %collective-permute-start.19) | collective-permute-done | bytes 786464 | tf_op jit(solution)/shard_map/ppermute | solution.py:37
  172.2 17.3 %collective-permute-done.20 = f32[2,2,48,512]{3,2,1,0:T(8,128)S(1)} collective-permute-done((f32[2,2,48,512]{3,2,1,0:T(8,128)S(1)}, f32[2,2,48,512]{3,2,1,0:T(8,128)S(1)}, u32[]{:S(2)}, u32[]{:S(2)}) %collective-permute-start.20) | collective-permute-done | bytes 393248 | tf_op jit(solution)/shard_map/ppermute | solution.py:37
  203.9 6.4 %collective-permute-done.16 = f32[2,2,48,768]{3,2,1,0:T(8,128)} collective-permute-done((f32[2,2,48,768]{3,2,1,0:T(8,128)}, f32[2,2,48,768]{3,2,1,0:T(8,128)}, u32[]{:S(2)}, u32[]{:S(2)}) %collective-permute-start.16) | collective-permute-done | bytes 589856 | tf_op jit(solution)/shard_map/ppermute | solution.py:37
  213.2 4.5 %collective-permute-done.12 = f32[2,2,48,1024]{3,2,1,0:T(8,128)} collective-permute-done((f32[2,2,48,1024]{3,2,1,0:T(8,128)}, f32[2,2,48,1024]{3,2,1,0:T(8,128)}, u32[]{:S(2)}, u32[]{:S(2)}) %collective-permute-start.12) | collective-permute-done | bytes 786464 | tf_op jit(solution)/shard_map/ppermute | solution.py:37
  220.9 3.4 %collective-permute-start.18 = (f32[48,768]{1,0:T(8,128)S(1)}, f32[48,768]{1,0:T(8,128)S(1)}, u32[]{:S(2)}, u32[]{:S(2)}) collective-permute-start(f32[48,768]{1,0:T(8,128)S(1)} %dynamic-slice_bitcast_fusion.11), channel_id=1, source_target_pairs={{0,16},{4,20},{8,24},{12,28},{16,0},{20,4},{24,8},{28,12},{1,17},{... | collective-permute-start | bytes 442376 | tf_op jit(solution)/shard_map/ppermute | solution.py:37
  224.4 6.9 %collective-permute-done.13 = f32[2,48,1024]{2,1,0:T(8,128)S(1)} collective-permute-done((f32[2,48,1024]{2,1,0:T(8,128)S(1)}, f32[2,48,1024]{2,1,0:T(8,128)S(1)}, u32[]{:S(2)}, u32[]{:S(2)}) %collective-permute-start.13) | collective-permute-done | bytes 393248 | tf_op jit(solution)/shard_map/ppermute | solution.py:37
  233.8 8.4 %collective-permute-done.14 = f32[48,1024]{1,0:T(8,128)S(1)} collective-permute-done((f32[48,1024]{1,0:T(8,128)S(1)}, f32[48,1024]{1,0:T(8,128)S(1)}, u32[]{:S(2)}, u32[]{:S(2)}) %collective-permute-start.14) | collective-permute-done | bytes 196640 | tf_op jit(solution)/shard_map/ppermute | solution.py:37
  (141 shorter events, 73.8 us)
Async XLA Ops:
  13.9 11.5 %collective-permute-start = (f32[]{:T(128)}, f32[]{:T(128)}, u32[]{:S(2)}, u32[]{:S(2)}) collective-permute-start(f32[]{:T(128)} %bitcast.2), channel_id=1, source_target_pairs={{0,4},{4,0},{8,12},{12,8},{16,20},{20,16},{24,28},{28,24},{1,5},{5... | collective-permute-start | bytes 20 | tf_op jit(solution)/shard_map/ppermute | solution.py:37
  26.6 3.7 %collective-permute-start.1 = (f32[]{:T(128)}, f32[]{:T(128)}, u32[]{:S(2)}, u32[]{:S(2)}) collective-permute-start(f32[]{:T(128)} %add.172), channel_id=1, source_target_pairs={{0,8},{4,12},{8,0},{12,4},{16,24},{20,28},{24,16},{28,20},{1,9},{5... | collective-permute-start | bytes 20 | tf_op jit(solution)/shard_map/ppermute | solution.py:37
  30.8 4.6 %collective-permute-start.2 = (f32[]{:T(128)}, f32[]{:T(128)}, u32[]{:S(2)}, u32[]{:S(2)}) collective-permute-start(f32[]{:T(128)} %add.173), channel_id=1, source_target_pairs={{0,16},{4,20},{8,24},{12,28},{16,0},{20,4},{24,8},{28,12},{1,17},{... | collective-permute-start | bytes 20 | tf_op jit(solution)/shard_map/ppermute | solution.py:37
  49.4 17.2 %collective-permute-start.7 = (bf16[2,12,72,256]{3,2,1,0:T(8,128)(2,1)S(1)}, bf16[2,12,72,256]{3,2,1,0:T(8,128)(2,1)S(1)}, u32[]{:S(2)}, u32[]{:S(2)}) collective-permute-start(bf16[2,12,72,256]{3,2,1,0:T(8,128)(2,1)S(1)} %bitcast.119), channel_id=1, source_target_pairs={{1,0},{2,1},{3,2},{5,4},{6,5},{7,6},{9,8},{10,9},{11,10},{13,12},{... | collective-permute-start | bytes 2654216 | tf_op jit(solution)/shard_map/ppermute | solution.py:20
  50.7 15.9 %collective-permute-start.6 = (bf16[2,12,72,256]{3,2,1,0:T(8,128)(2,1)S(1)}, bf16[2,12,72,256]{3,2,1,0:T(8,128)(2,1)S(1)}, u32[]{:S(2)}, u32[]{:S(2)}) collective-permute-start(bf16[2,12,72,256]{3,2,1,0:T(8,128)(2,1)S(1)} %bitcast.120), channel_id=1, source_target_pairs={{0,1},{1,2},{2,3},{4,5},{5,6},{6,7},{8,9},{9,10},{10,11},{12,13},{... | collective-permute-start | bytes 2654216 | tf_op jit(solution)/shard_map/ppermute | solution.py:19
  54.7 3.7 %collective-permute-start.3 = (f32[1281]{0:T(1024)S(1)}, f32[1281]{0:T(1024)S(1)}, u32[]{:S(2)}, u32[]{:S(2)}) collective-permute-start(f32[1281]{0:T(1024)S(1)} %constant_dynamic-update-slice_fusion.10), channel_id=1, source_target_pairs={{0,4},{4,0},{8,12},{12,8},{16,20},{20,16},{24,28},{28,24},{1,5},{5... | collective-permute-start | bytes 15380 | tf_op jit(solution)/shard_map/ppermute | solution.py:37
  58.4 3.7 %collective-permute-start.4 = (f32[1281]{0:T(1024)S(1)}, f32[1281]{0:T(1024)S(1)}, u32[]{:S(2)}, u32[]{:S(2)}) collective-permute-start(f32[1281]{0:T(1024)S(1)} %add.176), channel_id=1, source_target_pairs={{0,8},{4,12},{8,0},{12,4},{16,24},{20,28},{24,16},{28,20},{1,9},{5... | collective-permute-start | bytes 15380 | tf_op jit(solution)/shard_map/ppermute | solution.py:37
  62.1 4.5 %collective-permute-start.5 = (f32[1281]{0:T(1024)S(1)}, f32[1281]{0:T(1024)S(1)}, u32[]{:S(2)}, u32[]{:S(2)}) collective-permute-start(f32[1281]{0:T(1024)S(1)} %add.177), channel_id=1, source_target_pairs={{0,16},{4,20},{8,24},{12,28},{16,0},{20,4},{24,8},{28,12},{1,17},{... | collective-permute-start | bytes 15380 | tf_op jit(solution)/shard_map/ppermute | solution.py:37
  105.8 41.1 %collective-permute-start.8 = (f32[2,2,2,2,48,1024]{5,4,3,2,1,0:T(8,128)}, f32[2,2,2,2,48,1024]{5,4,3,2,1,0:T(8,128)}, u32[]{:S(2)}, u32[]{:S(2)}) collective-permute-start(f32[2,2,2,2,48,1024]{5,4,3,2,1,0:T(8,128)} %dynamic-slice_bitcast_fusion), channel_id=1, source_target_pairs={{0,1},{1,0},{2,3},{3,2},{4,5},{5,4},{6,7},{7,6},{8,9},{9,8},{10,11... | collective-permute-start | bytes 9437192 | tf_op jit(solution)/shard_map/ppermute | solution.py:37
  118.8 28.1 %collective-permute-start.10 = (f32[2,2,2,2,48,512]{5,4,3,2,1,0:T(8,128)}, f32[2,2,2,2,48,512]{5,4,3,2,1,0:T(8,128)}, u32[]{:S(2)}, u32[]{:S(2)}) collective-permute-start(f32[2,2,2,2,48,512]{5,4,3,2,1,0:T(8,128)} %dynamic-slice_bitcast_fusion.2), channel_id=1, source_target_pairs={{0,1},{1,0},{2,3},{3,2},{4,5},{5,4},{6,7},{7,6},{8,9},{9,8},{10,11... | collective-permute-start | bytes 4718600 | tf_op jit(solution)/shard_map/ppermute | solution.py:37
  127.2 19.6 %collective-permute-start.9 = (f32[2,2,2,2,48,768]{5,4,3,2,1,0:T(8,128)S(1)}, f32[2,2,2,2,48,768]{5,4,3,2,1,0:T(8,128)S(1)}, u32[]{:S(2)}, u32[]{:S(2)}) collective-permute-start(f32[2,2,2,2,48,768]{5,4,3,2,1,0:T(8,128)S(1)} %dynamic-slice_bitcast_fusion.1), channel_id=1, source_target_pairs={{0,1},{1,0},{2,3},{3,2},{4,5},{5,4},{6,7},{7,6},{8,9},{9,8},{10,11... | collective-permute-start | bytes 7077896 | tf_op jit(solution)/shard_map/ppermute | solution.py:37
  127.3 23.1 %slice-start.2 = ((s8[4718592]{0:T(1024)(128)(4,1)}), s8[4194304]{0:T(1024)(128)(4,1)S(1)}, s32[]{:S(2)}) async-start(s8[4718592]{0:T(1024)(128)(4,1)} %bitcast.113), calls=%async_computation.2 | async-start | bytes 8388608
  148.8 19.8 %collective-permute-start.19 = (f32[2,2,2,48,512]{4,3,2,1,0:T(8,128)S(1)}, f32[2,2,2,48,512]{4,3,2,1,0:T(8,128)S(1)}, u32[]{:S(2)}, u32[]{:S(2)}) collective-permute-start(f32[2,2,2,48,512]{4,3,2,1,0:T(8,128)S(1)} %dynamic-slice_bitcast_fusion.3), channel_id=1, source_target_pairs={{0,8},{4,12},{8,0},{12,4},{16,24},{20,28},{24,16},{28,20},{1,9},{5... | collective-permute-start | bytes 2359304 | tf_op jit(solution)/shard_map/ppermute | solution.py:37
  152.0 40.1 %collective-permute-start.15 = (f32[2,2,2,48,768]{4,3,1,0,2:T(8,128)}, f32[2,2,2,48,768]{4,3,1,0,2:T(8,128)}, u32[]{:S(2)}, u32[]{:S(2)}) collective-permute-start(f32[2,2,2,48,768]{4,3,1,0,2:T(8,128)} %bitcast.106), channel_id=1, source_target_pairs={{0,4},{4,0},{8,12},{12,8},{16,20},{20,16},{24,28},{28,24},{1,5},{5... | collective-permute-start | bytes 3538952 | tf_op jit(solution)/shard_map/ppermute | solution.py:37
  157.2 38.6 %collective-permute-start.11 = (f32[2,2,2,48,1024]{4,3,1,0,2:T(8,128)}, f32[2,2,2,48,1024]{4,3,1,0,2:T(8,128)}, u32[]{:S(2)}, u32[]{:S(2)}) collective-permute-start(f32[2,2,2,48,1024]{4,3,1,0,2:T(8,128)} %bitcast.105), channel_id=1, source_target_pairs={{0,2},{1,3},{2,0},{3,1},{4,6},{5,7},{6,4},{7,5},{8,10},{9,11},{10,... | collective-permute-start | bytes 4718600 | tf_op jit(solution)/shard_map/ppermute | solution.py:37
  169.6 19.9 %collective-permute-start.20 = (f32[2,2,48,512]{3,2,1,0:T(8,128)S(1)}, f32[2,2,48,512]{3,2,1,0:T(8,128)S(1)}, u32[]{:S(2)}, u32[]{:S(2)}) collective-permute-start(f32[2,2,48,512]{3,2,1,0:T(8,128)S(1)} %dynamic-slice_bitcast_fusion.6), channel_id=1, source_target_pairs={{0,16},{4,20},{8,24},{12,28},{16,0},{20,4},{24,8},{28,12},{1,17},{... | collective-permute-start | bytes 1179656 | tf_op jit(solution)/shard_map/ppermute | solution.py:37
  191.3 10.1 %collective-permute-start.21 = (f32[2,48,512]{2,1,0:T(8,128)}, f32[2,48,512]{2,1,0:T(8,128)}, u32[]{:S(2)}, u32[]{:S(2)}) collective-permute-start(f32[2,48,512]{2,1,0:T(8,128)} %dynamic-slice_bitcast_fusion.9), channel_id=1, source_target_pairs={{0,2},{1,3},{2,0},{3,1},{4,6},{5,7},{6,4},{7,5},{8,10},{9,11},{10,... | collective-permute-start | bytes 589832 | tf_op jit(solution)/shard_map/ppermute | solution.py:37
  194.5 15.9 %collective-permute-start.16 = (f32[2,2,48,768]{3,2,1,0:T(8,128)}, f32[2,2,48,768]{3,2,1,0:T(8,128)}, u32[]{:S(2)}, u32[]{:S(2)}) collective-permute-start(f32[2,2,48,768]{3,2,1,0:T(8,128)} %dynamic-slice_bitcast_fusion.5), channel_id=1, source_target_pairs={{0,2},{1,3},{2,0},{3,1},{4,6},{5,7},{6,4},{7,5},{8,10},{9,11},{10,... | collective-permute-start | bytes 1769480 | tf_op jit(solution)/shard_map/ppermute | solution.py:37
  198.5 19.2 %collective-permute-start.12 = (f32[2,2,48,1024]{3,2,1,0:T(8,128)}, f32[2,2,48,1024]{3,2,1,0:T(8,128)}, u32[]{:S(2)}, u32[]{:S(2)}) collective-permute-start(f32[2,2,48,1024]{3,2,1,0:T(8,128)} %dynamic-slice_bitcast_fusion.4), channel_id=1, source_target_pairs={{0,4},{4,0},{8,12},{12,8},{16,20},{20,16},{24,28},{28,24},{1,5},{5... | collective-permute-start | bytes 2359304 | tf_op jit(solution)/shard_map/ppermute | solution.py:37
  202.3 18.5 %collective-permute-start.22 = (f32[48,512]{1,0:T(8,128)S(1)}, f32[48,512]{1,0:T(8,128)S(1)}, u32[]{:S(2)}, u32[]{:S(2)}) collective-permute-start(f32[48,512]{1,0:T(8,128)S(1)} %dynamic-slice_bitcast_fusion.12), channel_id=1, source_target_pairs={{0,4},{4,0},{8,12},{12,8},{16,20},{20,16},{24,28},{28,24},{1,5},{5... | collective-permute-start | bytes 294920 | tf_op jit(solution)/shard_map/ppermute | solution.py:37
  211.6 9.3 %collective-permute-start.17 = (f32[2,48,768]{2,1,0:T(8,128)S(1)}, f32[2,48,768]{2,1,0:T(8,128)S(1)}, u32[]{:S(2)}, u32[]{:S(2)}) collective-permute-start(f32[2,48,768]{2,1,0:T(8,128)S(1)} %dynamic-slice_bitcast_fusion.8), channel_id=1, source_target_pairs={{0,8},{4,12},{8,0},{12,4},{16,24},{20,28},{24,16},{28,20},{1,9},{5... | collective-permute-start | bytes 884744 | tf_op jit(solution)/shard_map/ppermute | solution.py:37
  219.0 12.3 %collective-permute-start.13 = (f32[2,48,1024]{2,1,0:T(8,128)S(1)}, f32[2,48,1024]{2,1,0:T(8,128)S(1)}, u32[]{:S(2)}, u32[]{:S(2)}) collective-permute-start(f32[2,48,1024]{2,1,0:T(8,128)S(1)} %dynamic-slice_bitcast_fusion.7), channel_id=1, source_target_pairs={{0,8},{4,12},{8,0},{12,4},{16,24},{20,28},{24,16},{28,20},{1,9},{5... | collective-permute-start | bytes 1179656 | tf_op jit(solution)/shard_map/ppermute | solution.py:37
  220.9 12.8 %collective-permute-start.18 = (f32[48,768]{1,0:T(8,128)S(1)}, f32[48,768]{1,0:T(8,128)S(1)}, u32[]{:S(2)}, u32[]{:S(2)}) collective-permute-start(f32[48,768]{1,0:T(8,128)S(1)} %dynamic-slice_bitcast_fusion.11), channel_id=1, source_target_pairs={{0,16},{4,20},{8,24},{12,28},{16,0},{20,4},{24,8},{28,12},{1,17},{... | collective-permute-start | bytes 442376 | tf_op jit(solution)/shard_map/ppermute | solution.py:37
  231.4 10.8 %collective-permute-start.14 = (f32[48,1024]{1,0:T(8,128)S(1)}, f32[48,1024]{1,0:T(8,128)S(1)}, u32[]{:S(2)}, u32[]{:S(2)}) collective-permute-start(f32[48,1024]{1,0:T(8,128)S(1)} %dynamic-slice_bitcast_fusion.10), channel_id=1, source_target_pairs={{0,16},{4,20},{8,24},{12,28},{16,0},{20,4},{24,8},{28,12},{1,17},{... | collective-permute-start | bytes 589832 | tf_op jit(solution)/shard_map/ppermute | solution.py:37
  (14 other events, 181.3 us)

commit v5 on v4

--- a/solution.py
+++ b/solution.py
@@ -133,7 +133,6 @@
         piece = extended[:, row_off : row_off + tile_rows, col_off : col_off + columns, :]
         shifted_list.append(piece.reshape(local_pix, out_chans))
     shifted = jnp.concatenate(shifted_list, 1)
-    packed, shifted = lax.optimization_barrier((packed, shifted))
     grad_shift = packed[:out_chans]
     grad_gain = packed[out_chans : 2 * out_chans]
     grad_class = packed[2 * out_chans : (2 + classes) * out_chans].reshape(classes, out_chans)
@@ -143,10 +142,11 @@
     nbits = blocks.bit_length() - 1
     rows = in_chans // blocks
     flat_x = features.reshape(local_pix, in_chans)
+    packed, flat_x = lax.optimization_barrier((packed, flat_x))
     bits = [(axis, bit, combined) for combined, (axis, bit) in enumerate(index_bits(("rep", "tile")))]
     rest = bits[1:]
-    orders = [rest, rest[1:2] + rest[:1] + rest[2:], rest[2:] + rest[:2]]
-    group_taps = [taps - 2 * (taps // 3) + 1, taps // 3, taps // 3 - 1]
+    orders = [rest[s:] + rest[:s] for s in range(3)]
+    group_taps = [taps - 2 * (taps // 3), taps // 3, taps // 3]
     starts = [sum(group_taps[:s]) for s in range(3)]
     parts = []
     for s in range(3):
@@ -172,9 +172,21 @@
         ([exchange(v, axis, bit) for v in sends], accum_grad)
     )
     bit_axes.pop(ax)
-    pieces = []
-    for s in range(3):
-        pieces.append(halving_scatter(keeps[s] + received[s], orders[s], bit_axes))
+    pieces = [keeps[s] + received[s] for s in range(3)]
+    axes_of = [list(bit_axes) for s in range(3)]
+    for step in range(len(rest)):
+        sends, keeps = [], []
+        for s in range(3):
+            axis, bit, combined = orders[s][step]
+            ax = axes_of[s].index(combined)
+            mine = (lax.axis_index(axis) >> bit) & 1
+            keeps.append(lax.dynamic_index_in_dim(pieces[s], mine, ax, keepdims=False))
+            sends.append(lax.dynamic_index_in_dim(pieces[s], 1 - mine, ax, keepdims=False))
+            axes_of[s].pop(ax)
+        received = lax.optimization_barrier(
+            [exchange(sends[s], orders[s][step][0], orders[s][step][1]) for s in range(3)]
+        )
+        pieces = [keeps[s] + received[s] for s in range(3)]
     grad_weight = jnp.concatenate(pieces, 1).reshape(rows, taps, out_chans)
 
     grad_features = accum_grad.astype(jnp.bfloat16).reshape(images, tile_rows, columns, in_chans)

time: 245 us -> 218 us (0.89)
  local copies, waits for them, and re-layouts: 50.4 us -> 23.7 us
  waiting for transfers between devices: 62.9 us -> 75.2 us
  starting transfers between devices: 37.1 us -> 30.2 us
  other arithmetic: 23.5 us -> 20.2 us
  matrix products: 44.4 us -> 41.9 us
    dot_general x3 -> x0, local copies, waits for them, and re-layouts: 15.1 us -> none  [body(): lax.dot_general(flat_x, cols, (((0,), (0,)), ((), ())), preferred_element...]
    ppermute x21, waiting for transfers between devices: 62.9 us -> 75.2 us  [exchange(): return lax.ppermute(x, axis, pairs)]
    optimization_barrier x1 -> x0, local copies, waits for them, and re-layouts: 11.6 us -> none  [body(): packed, shifted = lax.optimization_barrier((packed, shifted))]
    ppermute x21, starting transfers between devices: 32.6 us -> 27.2 us  [exchange(): return lax.ppermute(x, axis, pairs)]
    squeeze x13 -> x12, local copies, waits for them, and re-layouts: 9.95 us -> 6.15 us  [body(): lax.dynamic_index_in_dim(pieces[s], 1 - mine, ax, keepdims=False)]
    add x15 -> x14, other arithmetic: 13.1 us -> 9.69 us  [body(): pieces = [keeps[s] + received[s] for s in range(3)]]
    unnamed x41 -> x35, local copies, waits for them, and re-layouts: 6.44 us -> 9.3 us
  transfers between devices with their start and end apart: 23 -> 23, of which waited for: 11 -> 16; matrix products, arithmetic and copies ran while one was open for 26% -> 25% of each run, Pallas kernels for 0% -> 0%
where the time goes in v5:
time: 218 us; the launch traced here: 217 us
  waiting for transfers between devices  75.2 us (34%)
  matrix products  41.9 us (19%)
  starting transfers between devices  30.2 us (14%)
  local copies, waits for them, and re-layouts  23.7 us (11%)
  blocking collectives  20.7 us (9%)
  other arithmetic  20.2 us (9%)
  between operations  5.45 us (2%)
    ppermute x21, waiting for transfers between devices, exchange(): return lax.ppermute(x, axis, pairs)  75.2 us
    ppermute x21, starting transfers between devices, exchange(): return lax.ppermute(x, axis, pairs)  27.2 us
    dot_general x1, matrix products, body(): lax.dot_general(shifted.reshape(local_pix, taps, out_chans), conv_weight,...  18 us
    dot_general x3, matrix products, body(): lax.dot_general(flat_x, cols, (((0,), (0,)), ((), ())), preferred_element...  17.9 us
    add x14, other arithmetic, body(): pieces = [keeps[s] + received[s] for s in range(3)]  9.69 us
    unnamed x35, local copies, waits for them, and re-layouts  9.3 us
    psum x1, blocking collectives, body(): lax.psum(jnp.concatenate([jnp.sum(yvals, 0), jnp.sum(weights_pix)[None]])...  8.37 us
    psum x1, blocking collectives, body(): lax.psum((jnp.sum(preactivation_gradient, 0), jnp.sum(preactivation_gradi...  6.48 us
  transfers between devices with their start and end apart: 23, of which 16 were waited for; matrix products, arithmetic and copies ran while one was open for 25% of the time, Pallas kernels for 0%

profile of v5, /device:TPU:0, one launch (start us, length us, event | category | flops | bytes accessed | tf_op | source)
XLA Modules:
  0.0 217.3 jit_solution(1370749147573511146)
XLA Ops:
  5.0 8.4 %psum.42 = f32[257]{0:T(512)S(1)} all-reduce(f32[257]{0:T(512)S(1)} %pad_maximum_fusion.1), channel_id=1, replica_groups=mesh['rep'=8,'tile'=4] {'tile'}, use_global_device_ids=true, to_apply=%region_2.0 | all-reduce | flops 257 | bytes 2056 | tf_op jit(solution)/shard_map/psum | solution.py:83
  16.8 5.8 %psum.43 = f32[256]{0:T(256)S(1)} all-reduce(f32[256]{0:T(256)S(1)} %multiply_reduce_fusion.1), channel_id=1, replica_groups=mesh['rep'=8,'tile'=4] {'tile'}, use_global_device_ids=true, to_apply=%region_4.0 | all-reduce | flops 256 | bytes 2048 | tf_op jit(solution)/shard_map/psum | solution.py:87
  26.7 2.9 %collective-permute-start.1 = (f32[]{:T(128)}, f32[]{:T(128)}, u32[]{:S(2)}, u32[]{:S(2)}) collective-permute-start(f32[]{:T(128)} %add.167), channel_id=1, source_target_pairs={{0,8},{4,12},{8,0},{12,4},{16,24},{20,28},{24,16},{28,20},{1,9},{5... | collective-permute-start | bytes 20 | tf_op jit(solution)/shard_map/ppermute | solution.py:37
  31.0 4.0 %collective-permute-start.2 = (f32[]{:T(128)}, f32[]{:T(128)}, u32[]{:S(2)}, u32[]{:S(2)}) collective-permute-start(f32[]{:T(128)} %add.168), channel_id=1, source_target_pairs={{0,16},{4,20},{8,24},{12,28},{16,0},{20,4},{24,8},{28,12},{1,17},{... | collective-permute-start | bytes 20 | tf_op jit(solution)/shard_map/ppermute | solution.py:37
  37.9 3.3 %multiply_reduce_fusion = (f32[256]{0:T(256)S(1)}, f32[256]{0:T(256)S(1)}, f32[1728,256]{1,0:T(8,128)}) fusion(f32[256]{0:T(256)S(1)} %get-tuple-element.80, f32[256]{0:T(256)S(1)} %slice_multiply_fusion, bf16[2,12,72,256]{3,2,1,0:T(8,128)(2,1)S(1)} %copy-done.2, f32[3,256]{1,0:T(4,128)S(1)} %copy-done, f32[1728,3]{0,1:T(4,128)S(1)} %get-tuple-element.84, ...), kind=kOutput, calls=%fused_computation.37 | convolution fusion | flops 20374336 | bytes 4474368 | tf_op jit(solution)/shard_map/dot_general | solution.py:100
  41.2 6.5 %all-reduce.1 = (f32[256]{0:T(256)S(1)}, f32[256]{0:T(256)S(1)}, f32[768]{0:T(1024)S(1)}, f32[1]{0:T(128)}) all-reduce(f32[256]{0:T(256)S(1)} %get-tuple-element.53, f32[256]{0:T(256)S(1)} %get-tuple-element.52, f32[768]{0:T(1024)S(1)} %reshape.111, f32[1]{0:T(128)} %bitcast.3), channel_id=1, replica_groups=mesh['rep'=8,'tile'=4] {'tile'}, use_global_device_ids=true, to_apply=%region_9.10 | all-reduce | flops 1281 | bytes 10248 | tf_op jit(solution)/shard_map/psum | solution.py:102
  53.8 3.2 %collective-permute-done.3 = f32[1281]{0:T(1024)S(1)} collective-permute-done((f32[1281]{0:T(1024)S(1)}, f32[1281]{0:T(1024)S(1)}, u32[]{:S(2)}, u32[]{:S(2)}) %collective-permute-start.3) | collective-permute-done | bytes 5156 | tf_op jit(solution)/shard_map/ppermute | solution.py:37
  58.6 2.1 collective-permute-done.4
  60.7 2.6 %collective-permute-start.5 = (f32[1281]{0:T(1024)S(1)}, f32[1281]{0:T(1024)S(1)}, u32[]{:S(2)}, u32[]{:S(2)}) collective-permute-start(f32[1281]{0:T(1024)S(1)} %add.172), channel_id=1, source_target_pairs={{0,16},{4,20},{8,24},{12,28},{16,0},{20,4},{24,8},{28,12},{1,17},{... | collective-permute-start | bytes 15380 | tf_op jit(solution)/shard_map/ppermute | solution.py:37
  65.3 2.1 fusion.5
  72.8 4.6 %fusion.18 = f32[1536,768]{1,0:T(8,128)S(1)} fusion(bf16[1728,1536]{1,0:T(8,128)(2,1)S(1)} %bitcast.142, bf16[1728,256]{1,0:T(8,128)(2,1)S(1)} %bitcast.122, bf16[1728,256]{1,0:T(8,128)(2,1)S(1)} %bitcast.118, bf16[1728,256]{1,0:T(8,128)(2,1)S(1)} %bitcast.124), kind=kOutput, calls=%fused_computation.22 | convolution fusion | flops 4084826112 | bytes 12681216 | tf_op jit(solution)/shard_map/dot_general | solution.py:154
  78.7 6.6 %fusion.12 = f32[1536,768]{1,0:T(8,128)S(1)} fusion(bf16[1728,1536]{1,0:T(8,128)(2,1)} %bitcast.138, bf16[1728,256]{1,0:T(8,128)(2,1)S(1)} %bitcast.126, bf16[1728,256]{1,0:T(8,128)(2,1)S(1)} %multiply_convert_fusion, bf16[1728,256]{1,0:T(8,128)(2,1)S(1)} %bitcast.133), kind=kOutput, calls=%fused_computation.16 | convolution fusion | flops 4084826112 | bytes 12681216 | tf_op jit(solution)/shard_map/dot_general | solution.py:154
  85.9 6.8 %fusion.6 = f32[1536,768]{1,0:T(8,128)S(1)} fusion(bf16[1728,1536]{1,0:T(8,128)(2,1)} %bitcast.139, bf16[1728,256]{1,0:T(8,128)(2,1)S(1)} %bitcast.129, bf16[1728,256]{1,0:T(8,128)(2,1)S(1)} %bitcast.121, bf16[1728,256]{1,0:T(8,128)(2,1)S(1)} %bitcast.131), kind=kOutput, calls=%fused_computation.10 | convolution fusion | flops 4084826112 | bytes 12681216 | tf_op jit(solution)/shard_map/dot_general | solution.py:154
  99.1 18.0 %convolution_bitcast_fusion = bf16[1728,1536]{1,0:T(8,128)(2,1)} fusion(bf16[1728,9,256]{2,0,1:T(8,128)(2,1)} %constant_dynamic-update-slice_fusion.1, bf16[9,1536,256]{2,1,0:T(8,128)(2,1)} %param.10), kind=kOutput, calls=%fused_computation.2 | convolution fusion | flops 12230590464 | bytes 20348928 | tf_op jit(solution)/shard_map/dot_general | solution.py:159
  123.4 2.0 collective-permute-start.11
  125.4 20.1 %collective-permute-done.13 = f32[2,2,2,48,768]{4,3,2,1,0:T(8,128)} collective-permute-done((f32[2,2,2,48,768]{4,3,2,1,0:T(8,128)S(1)}, f32[2,2,2,48,768]{4,3,2,1,0:T(8,128)}, u32[]{:S(2)}, u32[]{:S(2)}) %collective-permute-start.13) | collective-permute-done | bytes 1179680 | tf_op jit(solution)/shard_map/ppermute | solution.py:37
  145.6 3.1 %collective-permute-done.12 = f32[2,2,2,48,768]{4,3,2,1,0:T(8,128)} collective-permute-done((f32[2,2,2,48,768]{4,3,2,1,0:T(8,128)}, f32[2,2,2,48,768]{4,3,2,1,0:T(8,128)}, u32[]{:S(2)}, u32[]{:S(2)}) %collective-permute-start.12) | collective-permute-done | bytes 1179680 | tf_op jit(solution)/shard_map/ppermute | solution.py:37
  148.7 3.2 %collective-permute-done.11 = f32[2,2,2,48,768]{4,3,2,1,0:T(8,128)} collective-permute-done((f32[2,2,2,48,768]{4,3,2,1,0:T(8,128)}, f32[2,2,2,48,768]{4,3,2,1,0:T(8,128)}, u32[]{:S(2)}, u32[]{:S(2)}) %collective-permute-start.11) | collective-permute-done | bytes 1179680 | tf_op jit(solution)/shard_map/ppermute | solution.py:37
  154.2 2.6 %collective-permute-start.16 = (f32[2,2,48,768]{3,2,1,0:T(8,128)}, f32[2,2,48,768]{3,2,1,0:T(8,128)}, u32[]{:S(2)}, u32[]{:S(2)}) collective-permute-start(f32[2,2,48,768]{3,2,1,0:T(8,128)} %dynamic-slice_bitcast_fusion.3), channel_id=1, source_target_pairs={{0,16},{4,20},{8,24},{12,28},{16,0},{20,4},{24,8},{28,12},{1,17},{... | collective-permute-start | bytes 1769480 | tf_op jit(solution)/shard_map/ppermute | solution.py:37
  163.3 19.5 %collective-permute-done.16 = f32[2,2,48,768]{3,2,1,0:T(8,128)} collective-permute-done((f32[2,2,48,768]{3,2,1,0:T(8,128)}, f32[2,2,48,768]{3,2,1,0:T(8,128)}, u32[]{:S(2)}, u32[]{:S(2)}) %collective-permute-start.16) | collective-permute-done | bytes 589856 | tf_op jit(solution)/shard_map/ppermute | solution.py:37
  182.8 3.5 %collective-permute-done.15 = f32[2,2,48,768]{3,2,1,0:T(8,128)} collective-permute-done((f32[2,2,48,768]{3,2,1,0:T(8,128)}, f32[2,2,48,768]{3,2,1,0:T(8,128)}, u32[]{:S(2)}, u32[]{:S(2)}) %collective-permute-start.15) | collective-permute-done | bytes 589856 | tf_op jit(solution)/shard_map/ppermute | solution.py:37
  195.7 8.1 %collective-permute-done.18 = f32[2,48,768]{2,1,0:T(8,128)S(1)} collective-permute-done((f32[2,48,768]{2,1,0:T(8,128)S(1)}, f32[2,48,768]{2,1,0:T(8,128)S(1)}, u32[]{:S(2)}, u32[]{:S(2)}) %collective-permute-start.18) | collective-permute-done | bytes 294944 | tf_op jit(solution)/shard_map/ppermute | solution.py:37
  209.2 2.0 collective-permute-done.22
  212.7 2.5 %collective-permute-done.20 = f32[48,768]{1,0:T(8,128)S(1)} collective-permute-done((f32[48,768]{1,0:T(8,128)S(1)}, f32[48,768]{1,0:T(8,128)S(1)}, u32[]{:S(2)}, u32[]{:S(2)}) %collective-permute-start.20) | collective-permute-done | bytes 147488 | tf_op jit(solution)/shard_map/ppermute | solution.py:37
  (129 shorter events, 68.4 us)
Async XLA Ops:
  13.9 11.5 %collective-permute-start = (f32[]{:T(128)}, f32[]{:T(128)}, u32[]{:S(2)}, u32[]{:S(2)}) collective-permute-start(f32[]{:T(128)} %bitcast.2), channel_id=1, source_target_pairs={{0,4},{4,0},{8,12},{12,8},{16,20},{20,16},{24,28},{28,24},{1,5},{5... | collective-permute-start | bytes 20 | tf_op jit(solution)/shard_map/ppermute | solution.py:37
  26.7 3.7 %collective-permute-start.1 = (f32[]{:T(128)}, f32[]{:T(128)}, u32[]{:S(2)}, u32[]{:S(2)}) collective-permute-start(f32[]{:T(128)} %add.167), channel_id=1, source_target_pairs={{0,8},{4,12},{8,0},{12,4},{16,24},{20,28},{24,16},{28,20},{1,9},{5... | collective-permute-start | bytes 20 | tf_op jit(solution)/shard_map/ppermute | solution.py:37
  31.0 4.6 %collective-permute-start.2 = (f32[]{:T(128)}, f32[]{:T(128)}, u32[]{:S(2)}, u32[]{:S(2)}) collective-permute-start(f32[]{:T(128)} %add.168), channel_id=1, source_target_pairs={{0,16},{4,20},{8,24},{12,28},{16,0},{20,4},{24,8},{28,12},{1,17},{... | collective-permute-start | bytes 20 | tf_op jit(solution)/shard_map/ppermute | solution.py:37
  49.6 15.6 %collective-permute-start.6 = (bf16[2,12,72,256]{3,2,1,0:T(8,128)(2,1)S(1)}, bf16[2,12,72,256]{3,2,1,0:T(8,128)(2,1)S(1)}, u32[]{:S(2)}, u32[]{:S(2)}) collective-permute-start(bf16[2,12,72,256]{3,2,1,0:T(8,128)(2,1)S(1)} %bitcast.112), channel_id=1, source_target_pairs={{0,1},{1,2},{2,3},{4,5},{5,6},{6,7},{8,9},{9,10},{10,11},{12,13},{... | collective-permute-start | bytes 2654216 | tf_op jit(solution)/shard_map/ppermute | solution.py:19
  51.3 13.9 %collective-permute-start.7 = (bf16[2,12,72,256]{3,2,1,0:T(8,128)(2,1)S(1)}, bf16[2,12,72,256]{3,2,1,0:T(8,128)(2,1)S(1)}, u32[]{:S(2)}, u32[]{:S(2)}) collective-permute-start(bf16[2,12,72,256]{3,2,1,0:T(8,128)(2,1)S(1)} %bitcast.113), channel_id=1, source_target_pairs={{1,0},{2,1},{3,2},{5,4},{6,5},{7,6},{9,8},{10,9},{11,10},{13,12},{... | collective-permute-start | bytes 2654216 | tf_op jit(solution)/shard_map/ppermute | solution.py:20
  53.3 3.7 %collective-permute-start.3 = (f32[1281]{0:T(1024)S(1)}, f32[1281]{0:T(1024)S(1)}, u32[]{:S(2)}, u32[]{:S(2)}) collective-permute-start(f32[1281]{0:T(1024)S(1)} %constant_dynamic-update-slice_fusion.9), channel_id=1, source_target_pairs={{0,4},{4,0},{8,12},{12,8},{16,20},{20,16},{24,28},{28,24},{1,5},{5... | collective-permute-start | bytes 15380 | tf_op jit(solution)/shard_map/ppermute | solution.py:37
  57.0 3.7 %collective-permute-start.4 = (f32[1281]{0:T(1024)S(1)}, f32[1281]{0:T(1024)S(1)}, u32[]{:S(2)}, u32[]{:S(2)}) collective-permute-start(f32[1281]{0:T(1024)S(1)} %add.171), channel_id=1, source_target_pairs={{0,8},{4,12},{8,0},{12,4},{16,24},{20,28},{24,16},{28,20},{1,9},{5... | collective-permute-start | bytes 15380 | tf_op jit(solution)/shard_map/ppermute | solution.py:37
  60.7 4.5 %collective-permute-start.5 = (f32[1281]{0:T(1024)S(1)}, f32[1281]{0:T(1024)S(1)}, u32[]{:S(2)}, u32[]{:S(2)}) collective-permute-start(f32[1281]{0:T(1024)S(1)} %add.172), channel_id=1, source_target_pairs={{0,16},{4,20},{8,24},{12,28},{16,0},{20,4},{24,8},{28,12},{1,17},{... | collective-permute-start | bytes 15380 | tf_op jit(solution)/shard_map/ppermute | solution.py:37
  77.9 39.2 %collective-permute-start.10 = (f32[2,2,2,2,48,768]{5,4,3,2,0,1:T(8,128)S(1)}, f32[2,2,2,2,48,768]{5,4,3,2,0,1:T(8,128)S(1)}, u32[]{:S(2)}, u32[]{:S(2)}) collective-permute-start(f32[2,2,2,2,48,768]{5,4,3,2,0,1:T(8,128)S(1)} %bitcast.134), channel_id=1, source_target_pairs={{0,1},{1,0},{2,3},{3,2},{4,5},{5,4},{6,7},{7,6},{8,9},{9,8},{10,11... | collective-permute-start | bytes 7077896 | tf_op jit(solution)/shard_map/ppermute | solution.py:37
  85.8 31.3 %collective-permute-start.9 = (f32[2,2,2,2,48,768]{5,4,3,1,0,2:T(8,128)S(1)}, f32[2,2,2,2,48,768]{5,4,3,1,0,2:T(8,128)S(1)}, u32[]{:S(2)}, u32[]{:S(2)}) collective-permute-start(f32[2,2,2,2,48,768]{5,4,3,1,0,2:T(8,128)S(1)} %bitcast.135), channel_id=1, source_target_pairs={{0,1},{1,0},{2,3},{3,2},{4,5},{5,4},{6,7},{7,6},{8,9},{9,8},{10,11... | collective-permute-start | bytes 7077896 | tf_op jit(solution)/shard_map/ppermute | solution.py:37
  94.6 22.5 %collective-permute-start.8 = (f32[2,2,2,2,48,768]{5,4,2,1,0,3:T(8,128)}, f32[2,2,2,2,48,768]{5,4,2,1,0,3:T(8,128)S(1)}, u32[]{:S(2)}, u32[]{:S(2)}) collective-permute-start(f32[2,2,2,2,48,768]{5,4,2,1,0,3:T(8,128)} %bitcast.110), channel_id=1, source_target_pairs={{0,1},{1,0},{2,3},{3,2},{4,5},{5,4},{6,7},{7,6},{8,9},{9,8},{10,11... | collective-permute-start | bytes 7077896 | tf_op jit(solution)/shard_map/ppermute | solution.py:37
  117.5 28.1 %collective-permute-start.13 = (f32[2,2,2,48,768]{4,3,2,1,0:T(8,128)S(1)}, f32[2,2,2,48,768]{4,3,2,1,0:T(8,128)}, u32[]{:S(2)}, u32[]{:S(2)}) collective-permute-start(f32[2,2,2,48,768]{4,3,2,1,0:T(8,128)S(1)} %dynamic-slice_bitcast_fusion), channel_id=1, source_target_pairs={{0,8},{4,12},{8,0},{12,4},{16,24},{20,28},{24,16},{28,20},{1,9},{5... | collective-permute-start | bytes 3538952 | tf_op jit(solution)/shard_map/ppermute | solution.py:37
  120.8 27.9 %collective-permute-start.12 = (f32[2,2,2,48,768]{4,3,2,1,0:T(8,128)}, f32[2,2,2,48,768]{4,3,2,1,0:T(8,128)}, u32[]{:S(2)}, u32[]{:S(2)}) collective-permute-start(f32[2,2,2,48,768]{4,3,2,1,0:T(8,128)} %dynamic-slice_bitcast_fusion.1), channel_id=1, source_target_pairs={{0,4},{4,0},{8,12},{12,8},{16,20},{20,16},{24,28},{28,24},{1,5},{5... | collective-permute-start | bytes 3538952 | tf_op jit(solution)/shard_map/ppermute | solution.py:37
  123.4 28.5 %collective-permute-start.11 = (f32[2,2,2,48,768]{4,3,2,1,0:T(8,128)}, f32[2,2,2,48,768]{4,3,2,1,0:T(8,128)}, u32[]{:S(2)}, u32[]{:S(2)}) collective-permute-start(f32[2,2,2,48,768]{4,3,2,1,0:T(8,128)} %dynamic-slice_bitcast_fusion.2), channel_id=1, source_target_pairs={{0,2},{1,3},{2,0},{3,1},{4,6},{5,7},{6,4},{7,5},{8,10},{9,11},{10,... | collective-permute-start | bytes 3538952 | tf_op jit(solution)/shard_map/ppermute | solution.py:37
  125.4 31.3 %copy-start.4 = (f32[2,2,2,2,48,768]{5,4,3,1,0,2:T(8,128)S(1)}, f32[2,2,2,2,48,768]{5,4,3,1,0,2:T(8,128)}, u32[]{:S(2)}) copy-start(f32[2,2,2,2,48,768]{5,4,3,1,0,2:T(8,128)} %copy-done.3) | copy-start | bytes 7077892
  154.2 28.6 %collective-permute-start.16 = (f32[2,2,48,768]{3,2,1,0:T(8,128)}, f32[2,2,48,768]{3,2,1,0:T(8,128)}, u32[]{:S(2)}, u32[]{:S(2)}) collective-permute-start(f32[2,2,48,768]{3,2,1,0:T(8,128)} %dynamic-slice_bitcast_fusion.3), channel_id=1, source_target_pairs={{0,16},{4,20},{8,24},{12,28},{16,0},{20,4},{24,8},{28,12},{1,17},{... | collective-permute-start | bytes 1769480 | tf_op jit(solution)/shard_map/ppermute | solution.py:37
  159.1 27.3 %collective-permute-start.15 = (f32[2,2,48,768]{3,2,1,0:T(8,128)}, f32[2,2,48,768]{3,2,1,0:T(8,128)}, u32[]{:S(2)}, u32[]{:S(2)}) collective-permute-start(f32[2,2,48,768]{3,2,1,0:T(8,128)} %dynamic-slice_bitcast_fusion.4), channel_id=1, source_target_pairs={{0,8},{4,12},{8,0},{12,4},{16,24},{20,28},{24,16},{28,20},{1,9},{5... | collective-permute-start | bytes 1769480 | tf_op jit(solution)/shard_map/ppermute | solution.py:37
  161.8 24.5 %collective-permute-start.14 = (f32[2,2,48,768]{3,2,1,0:T(8,128)}, f32[2,2,48,768]{3,2,1,0:T(8,128)}, u32[]{:S(2)}, u32[]{:S(2)}) collective-permute-start(f32[2,2,48,768]{3,2,1,0:T(8,128)} %dynamic-slice_bitcast_fusion.5), channel_id=1, source_target_pairs={{0,4},{4,0},{8,12},{12,8},{16,20},{20,16},{24,28},{28,24},{1,5},{5... | collective-permute-start | bytes 1769480 | tf_op jit(solution)/shard_map/ppermute | solution.py:37
  188.3 7.4 %collective-permute-start.19 = (f32[2,48,768]{2,1,0:T(8,128)}, f32[2,48,768]{2,1,0:T(8,128)S(1)}, u32[]{:S(2)}, u32[]{:S(2)}) collective-permute-start(f32[2,48,768]{2,1,0:T(8,128)} %dynamic-slice_bitcast_fusion.6), channel_id=1, source_target_pairs={{0,2},{1,3},{2,0},{3,1},{4,6},{5,7},{6,4},{7,5},{8,10},{9,11},{10,... | collective-permute-start | bytes 884744 | tf_op jit(solution)/shard_map/ppermute | solution.py:37
  190.9 12.9 %collective-permute-start.18 = (f32[2,48,768]{2,1,0:T(8,128)S(1)}, f32[2,48,768]{2,1,0:T(8,128)S(1)}, u32[]{:S(2)}, u32[]{:S(2)}) collective-permute-start(f32[2,48,768]{2,1,0:T(8,128)S(1)} %dynamic-slice_bitcast_fusion.7), channel_id=1, source_target_pairs={{0,16},{4,20},{8,24},{12,28},{16,0},{20,4},{24,8},{28,12},{1,17},{... | collective-permute-start | bytes 884744 | tf_op jit(solution)/shard_map/ppermute | solution.py:37
  192.1 12.9 %collective-permute-start.17 = (f32[2,48,768]{2,1,0:T(8,128)S(1)}, f32[2,48,768]{2,1,0:T(8,128)S(1)}, u32[]{:S(2)}, u32[]{:S(2)}) collective-permute-start(f32[2,48,768]{2,1,0:T(8,128)S(1)} %dynamic-slice_bitcast_fusion.8), channel_id=1, source_target_pairs={{0,8},{4,12},{8,0},{12,4},{16,24},{20,28},{24,16},{28,20},{1,9},{5... | collective-permute-start | bytes 884744 | tf_op jit(solution)/shard_map/ppermute | solution.py:37
  206.1 5.2 %collective-permute-start.22 = (f32[48,768]{1,0:T(8,128)S(1)}, f32[48,768]{1,0:T(8,128)S(1)}, u32[]{:S(2)}, u32[]{:S(2)}) collective-permute-start(f32[48,768]{1,0:T(8,128)S(1)} %dynamic-slice_bitcast_fusion.9), channel_id=1, source_target_pairs={{0,4},{4,0},{8,12},{12,8},{16,20},{20,16},{24,28},{28,24},{1,5},{5... | collective-permute-start | bytes 442376 | tf_op jit(solution)/shard_map/ppermute | solution.py:37
  207.5 5.2 %collective-permute-start.21 = (f32[48,768]{1,0:T(8,128)S(1)}, f32[48,768]{1,0:T(8,128)S(1)}, u32[]{:S(2)}, u32[]{:S(2)}) collective-permute-start(f32[48,768]{1,0:T(8,128)S(1)} %dynamic-slice_bitcast_fusion.10), channel_id=1, source_target_pairs={{0,2},{1,3},{2,0},{3,1},{4,6},{5,7},{6,4},{7,5},{8,10},{9,11},{10,... | collective-permute-start | bytes 442376 | tf_op jit(solution)/shard_map/ppermute | solution.py:37
  208.6 6.7 %collective-permute-start.20 = (f32[48,768]{1,0:T(8,128)S(1)}, f32[48,768]{1,0:T(8,128)S(1)}, u32[]{:S(2)}, u32[]{:S(2)}) collective-permute-start(f32[48,768]{1,0:T(8,128)S(1)} %dynamic-slice_bitcast_fusion.11), channel_id=1, source_target_pairs={{0,16},{4,20},{8,24},{12,28},{16,0},{20,4},{24,8},{28,12},{1,17},{... | collective-permute-start | bytes 442376 | tf_op jit(solution)/shard_map/ppermute | solution.py:37
  (11 other events, 127.0 us)
